TPU v7x, 1024 devices: a whole 4x8x16 slice. The times are simulated.
1024 devices in a mesh: dp: 32 (over z, core), expert: 32 (over y, x).
Axes of the slice: x: 4, y: 8, z: 16, core: 2. Of those that a mesh axis runs over, the one named last changes fastest.
Arguments:
- route_ids: int32 [131072, 2], P(('dp', 'expert')), may hold values from 0 to 31, all different within a row; in each aligned block of 128 rows (0 to 127, 128 to 255, ...) at most 10 rows name the same one
- gate_values: float32 [131072, 2], P(('dp', 'expert')), may hold values from 0.1 to 1
- out_grad: bfloat16 [131072, 2048], P(('dp', 'expert')), may hold values from -4 to 4
- down_weight: bfloat16 [32, 768, 2048], P('expert'), may hold values from -0.21875 to 0.21875
- hidden: bfloat16 [32, 32, 32, 10, 768], P('dp', 'expert'), may hold values from -6 to 6
Outputs:
- mixed_out: bfloat16 [131072, 2048], P(('dp', 'expert'))
- gate_grad: float32 [131072, 2], P(('dp', 'expert'))
- hidden_grad: bfloat16 [32, 32, 32, 10, 768], P('dp', 'expert')
- weight_grad: float32 [32, 768, 2048], P('expert', 'dp')
Inputs may be any that keep to these rules, and one draw needn't show every extreme that they name: `route_ids`: each row names 2 different experts. Among the rows of one device no expert is named by more than 10 rows, and in every draw some device names some expert exactly 10 times.
All inputs are finite; a program needn't handle non-finite values.
Results may differ from a plain program's by a relative error of at most 0.0049.
Values may be sent and summed in bfloat16 or wider, within the bound.
No kernel may reach another device: no remote copies, remote signals or barrier semaphores. Data moves between devices by JAX's collectives and lax.ppermute only.
A program may use at most 64 MiB of HBM per device.

v0:
```python
import jax
import jax.numpy as jnp
from jax import lax
from jax.sharding import PartitionSpec as P


def slot_table(route_ids, experts, capacity):
    flat_ids = route_ids.reshape(-1)
    route_count = flat_ids.shape[0]
    onehot = (flat_ids[:, None] == jnp.arange(experts, dtype=jnp.int32)[None, :]).astype(
        jnp.float32
    )
    positions = jnp.arange(route_count, dtype=jnp.int32)
    earlier = (positions[:, None] > positions[None, :]).astype(jnp.float32)
    before = jnp.dot(
        earlier, onehot, precision=lax.Precision.HIGHEST, preferred_element_type=jnp.float32
    )
    slot_rank = jnp.sum(before * onehot, axis=1).astype(jnp.int32)
    slot_index = flat_ids * capacity + slot_rank
    slots_all = jnp.arange(experts * capacity, dtype=jnp.int32)
    return (slots_all[:, None] == slot_index[None, :]).astype(jnp.bfloat16)


def on_device(route_ids, gate_values, out_grad, down_weight, hidden):
    experts = lax.axis_size("expert")
    capacity = hidden.shape[3]
    inner_width = hidden.shape[4]
    feature_width = out_grad.shape[1]
    tok_rows = route_ids.shape[0]
    routes = route_ids.shape[1]
    slot_map = slot_table(route_ids, experts, capacity)
    weight_mat = down_weight[0]
    rows_in = hidden.reshape(-1, inner_width)
    expert_out = jnp.dot(rows_in, weight_mat, preferred_element_type=jnp.float32)
    expert_out = expert_out.astype(jnp.bfloat16).reshape(experts, capacity, feature_width)
    grads_f = out_grad.astype(jnp.float32)
    scaled = (
        (gate_values[:, :, None] * grads_f[:, None, :])
        .reshape(-1, feature_width)
        .astype(jnp.bfloat16)
    )
    outgoing = jnp.dot(slot_map, scaled, preferred_element_type=jnp.float32)
    outgoing = outgoing.astype(jnp.bfloat16).reshape(experts, capacity, feature_width)
    returned = lax.all_to_all(expert_out, "expert", split_axis=0, concat_axis=0, tiled=True)
    incoming = lax.all_to_all(outgoing, "expert", split_axis=0, concat_axis=0, tiled=True)
    gathered = jnp.einsum(
        "sr,sd->rd",
        slot_map,
        returned.reshape(-1, feature_width),
        preferred_element_type=jnp.float32,
    )
    gathered = gathered.reshape(tok_rows, routes, feature_width)
    mixed_out = jnp.sum(gate_values[:, :, None] * gathered, axis=1).astype(jnp.bfloat16)
    gate_grad = jnp.sum(gathered * grads_f[:, None, :], axis=2)
    grad_rows = incoming.reshape(-1, feature_width)
    hidden_grad = jnp.einsum("sd,hd->sh", grad_rows, weight_mat, preferred_element_type=jnp.float32)
    hidden_grad = hidden_grad.astype(jnp.bfloat16).reshape(hidden.shape)
    partial_term = jnp.einsum("sh,sd->hd", rows_in, grad_rows, preferred_element_type=jnp.float32)
    weight_grad = lax.psum_scatter(partial_term, "dp", scatter_dimension=0, tiled=True)
    return (mixed_out, gate_grad, hidden_grad, weight_grad[None])


def solution(mesh):
    in_specs = (
        P(("dp", "expert"), None),
        P(("dp", "expert"), None),
        P(("dp", "expert"), None),
        P("expert", None, None),
        P("dp", "expert", None, None, None),
    )
    out_specs = (
        P(("dp", "expert"), None),
        P(("dp", "expert"), None),
        P("dp", "expert", None, None, None),
        P("expert", "dp", None),
    )
    return jax.shard_map(
        on_device, mesh=mesh, in_specs=in_specs, out_specs=out_specs, check_vma=False
    )
```

profile of v0, /device:TPU:6, one launch (start us, length us, event | category | flops | bytes accessed | tf_op | source)
XLA Modules:
  0.0 239.2 jit_solution(751767396114603120)
XLA Ops:
  9.4 3.4 %mul.50.clone = f32[128,2,2048]{2,1,0:T(2,128)} broadcast(bf16[128,2048]{1,0:T(8,128)(2,1)} %param.7), dimensions={0,2} | broadcast | bytes 2621440 | tf_op jit(solution)/shard_map/mul | solution.py:54
  12.8 3.7 %mul.54 = f32[256,2048]{1,0:T(8,128)} reshape(f32[128,2,2048]{2,1,0:T(2,128)} %mul.50.clone) | data formatting | bytes 4194304 | tf_op jit(solution)/shard_map/mul | solution.py:54
  16.5 3.2 %convolution_convert_fusion = bf16[320,2048]{1,0:T(8,128)(2,1)} fusion(f32[256,2048]{1,0:T(8,128)} %mul.54, f32[256]{0:T(256)S(1)} %mul.52, s32[256]{0:T(256)S(1)} %convert_add_fusion), kind=kOutput, calls=%fused_computation.6 | convolution fusion | flops 337330176 | bytes 3409920 | tf_op jit(solution)/shard_map/dot_general | solution.py:42
  19.8 3.3 %reshape.74 = bf16[32,10,2048]{2,1,0:T(8,128)(2,1)} reshape(bf16[320,2048]{1,0:T(8,128)(2,1)} %convolution_convert_fusion) | data formatting | bytes 2621440 | tf_op jit(solution)/shard_map/reshape | solution.py:43
  23.1 17.4 %all-to-all-start.1 = ((bf16[32,10,2048]{2,1,0:T(8,128)(2,1)}), bf16[32,10,2048]{2,1,0:T(8,128)(2,1)}, u32[]{:S(2)}, u32[]{:S(2)}) async-start(bf16[32,10,2048]{2,1,0:T(8,128)(2,1)} %reshape.74), calls=%async_computation.1 | async-start | bytes 4194304 | tf_op jit(solution)/shard_map/all_to_all | solution.py:45
  40.6 2.2 copy.19
  42.8 2.0 reshape.71
  44.8 38.5 %all-to-all-done.1 = bf16[32,10,2048]{2,1,0:T(8,128)(2,1)} async-done(((bf16[32,10,2048]{2,1,0:T(8,128)(2,1)}), bf16[32,10,2048]{2,1,0:T(8,128)(2,1)}, u32[]{:S(2)}, u32[]{:S(2)}) %all-to-all-start.1) | async-done | bytes 1310752 | tf_op jit(solution)/shard_map/all_to_all | solution.py:45
  83.3 3.6 %reshape.75 = bf16[320,2048]{1,0:T(8,128)(2,1)} reshape(bf16[32,10,2048]{2,1,0:T(8,128)(2,1)} %all-to-all-done.1) | data formatting | bytes 2621440 | tf_op jit(solution)/shard_map/reshape | solution.py:55
  86.8 5.9 %convolution_bitcast_fusion = f32[768,2048]{0,1:T(8,128)} fusion(bf16[320,2048]{1,0:T(8,128)(2,1)} %reshape.75, bf16[320,768]{1,0:T(8,128)(2,1)} %reshape.71), kind=kOutput, calls=%fused_computation | convolution fusion | flops 1006632960 | bytes 8093696 | tf_op jit(solution)/shard_map/sh,sd->hd/dot_general | solution.py:58
  92.8 6.6 %copy.25 = f32[768,2048]{1,0:T(8,128)} copy(f32[768,2048]{0,1:T(8,128)} %convolution_bitcast_fusion) | data formatting | bytes 12582912
  99.4 3.3 %fusion.4 = bf16[320,2048]{1,0:T(8,128)(2,1)} fusion(bf16[320,768]{1,0:T(8,128)(2,1)} %reshape.71, bf16[1,768,2048]{2,1,0:T(8,128)(2,1)S(1)} %copy-done), kind=kOutput, calls=%fused_computation.5 | convolution fusion | flops 1007288320 | bytes 4947968 | tf_op jit(solution)/shard_map/dot_general | solution.py:34
  102.7 3.3 %reshape.72 = bf16[32,10,2048]{2,1,0:T(8,128)(2,1)} reshape(bf16[320,2048]{1,0:T(8,128)(2,1)} %fusion.4) | data formatting | bytes 2621440 | tf_op jit(solution)/shard_map/reshape | solution.py:35
  106.0 6.3 %all-to-all-start = ((bf16[32,10,2048]{2,1,0:T(8,128)(2,1)}), bf16[32,10,2048]{2,1,0:T(8,128)(2,1)}, u32[]{:S(2)}, u32[]{:S(2)}) async-start(bf16[32,10,2048]{2,1,0:T(8,128)(2,1)} %reshape.72), calls=%async_computation | async-start | bytes 4194304 | tf_op jit(solution)/shard_map/all_to_all | solution.py:44
  112.3 2.1 convert_element_type.31
  114.7 3.3 %fusion.7 = bf16[320,768]{1,0:T(8,128)(2,1)} fusion(bf16[320,2048]{1,0:T(8,128)(2,1)} %reshape.75, bf16[1,768,2048]{2,1,0:T(8,128)(2,1)S(1)} %copy-done), kind=kOutput, calls=%fused_computation.10 | convolution fusion | flops 1006878720 | bytes 4947968 | tf_op jit(solution)/shard_map/sd,hd->sh/dot_general | solution.py:56
  118.0 2.0 reshape.76
  120.1 2.1 copy.23
  122.1 34.7 %all-to-all-done = bf16[32,10,2048]{2,1,0:T(8,128)(2,1)} async-done(((bf16[32,10,2048]{2,1,0:T(8,128)(2,1)}), bf16[32,10,2048]{2,1,0:T(8,128)(2,1)}, u32[]{:S(2)}, u32[]{:S(2)}) %all-to-all-start) | async-done | bytes 1310752 | tf_op jit(solution)/shard_map/all_to_all | solution.py:44
  156.8 3.6 %reshape.77 = bf16[320,2048,1]{1,0,2:T(8,128)(2,1)} reshape(bf16[32,10,2048]{2,1,0:T(8,128)(2,1)} %all-to-all-done) | data formatting | bytes 2621440 | tf_op jit(solution)/shard_map/reshape | solution.py:49
  160.4 3.4 %multiply_reduce_fusion = (f32[128,2]{0,1:T(2,128)}, bf16[128,2048]{1,0:T(8,128)(2,1)}) fusion(f32[128,2048]{1,0:T(8,128)} %convert_element_type.31, f32[128,2]{0,1:T(2,128)S(1)} %copy-done.1, bf16[320,2048,1]{1,0,2:T(8,128)(2,1)} %reshape.77, pred[128,2,320]{2,1,0:T(4,128)(4,1)S(1)} %eq.47), kind=kOutput, calls=%fused_computation.8 | convolution fusion | flops 337379072 | bytes 2967552 | tf_op jit(solution)/shard_map/sr,sd->rd/dot_general | solution.py:46
  163.8 64.0 %reduce-scatter.4.cloned.1.call-done = f32[24,2048]{1,0:T(8,128)} async-done(((f32[768,2048]{1,0:T(8,128)}), f32[24,2048]{1,0:T(8,128)}) %reduce-scatter.4.cloned.1.call-update) | async-done | bytes 196624
  227.8 2.3 copy.26
  230.1 2.2 copy.24
  (14 shorter events, 2.5 us)
Async XLA Ops:
  7.2 92.2 %copy-start = (bf16[1,768,2048]{2,1,0:T(8,128)(2,1)S(1)}, bf16[1,768,2048]{2,1,0:T(8,128)(2,1)}, u32[]{:S(2)}) copy-start(bf16[1,768,2048]{2,1,0:T(8,128)(2,1)} %param.8) | copy-start | bytes 9437188
  23.1 60.2 %all-to-all-start.1 = ((bf16[32,10,2048]{2,1,0:T(8,128)(2,1)}), bf16[32,10,2048]{2,1,0:T(8,128)(2,1)}, u32[]{:S(2)}, u32[]{:S(2)}) async-start(bf16[32,10,2048]{2,1,0:T(8,128)(2,1)} %reshape.74), calls=%async_computation.1 | async-start | bytes 4194304 | tf_op jit(solution)/shard_map/all_to_all | solution.py:45
  40.5 187.3 %reduce-scatter.4.cloned.1.call-start = ((), (), s32[]{:S(2)}) async-start(), calls=%async_computation.3 | async-start | bytes 6488064
  106.0 50.8 %all-to-all-start = ((bf16[32,10,2048]{2,1,0:T(8,128)(2,1)}), bf16[32,10,2048]{2,1,0:T(8,128)(2,1)}, u32[]{:S(2)}, u32[]{:S(2)}) async-start(bf16[32,10,2048]{2,1,0:T(8,128)(2,1)} %reshape.72), calls=%async_computation | async-start | bytes 4194304 | tf_op jit(solution)/shard_map/all_to_all | solution.py:44
  120.1 40.4 %copy-start.1 = (f32[128,2]{0,1:T(2,128)S(1)}, f32[128,2]{0,1:T(2,128)}, u32[]{:S(2)}) copy-start(f32[128,2]{0,1:T(2,128)} %param.6) | copy-start | bytes 3076
Sparse Core Ops, SparseCore 0:
  99.5 128.2 reduce-scatter.3
where the time goes:
time: 240 us; the launch traced here: 239 us
  waiting for transfers between devices  137 us (57%)
  local copies, waits for them, and re-layouts  42.5 us (18%)
  starting transfers between devices  23.8 us (10%)
  matrix products  19.4 us (8%)
  between operations  14.1 us (6%)
    unnamed x2, waiting for transfers between devices  64 us
    all_to_all x1, waiting for transfers between devices, on_device(): lax.all_to_all(outgoing, 'expert', split_axis=0, concat_axis=0, tiled=True)  38.5 us
    all_to_all x1, waiting for transfers between devices, on_device(): lax.all_to_all(expert_out, 'expert', split_axis=0, concat_axis=0, tiled=T...  34.7 us
    all_to_all x1, starting transfers between devices, on_device(): lax.all_to_all(outgoing, 'expert', split_axis=0, concat_axis=0, tiled=True)  17.4 us
    unnamed x11, local copies, waits for them, and re-layouts  17.1 us
    mul x2, local copies, waits for them, and re-layouts, on_device(): gate_grad = jnp.sum(gathered * grads_f[:, None, :], axis=2)  7.1 us
    all_to_all x1, starting transfers between devices, on_device(): lax.all_to_all(expert_out, 'expert', split_axis=0, concat_axis=0, tiled=T...  6.29 us
    dot_general x1, matrix products, on_device(): jnp.einsum('sh,sd->hd', rows_in, grad_rows, preferred_element_type=jnp.fl...  5.92 us
  transfers between devices with their start and end apart: 3, of which 3 were waited for; matrix products, arithmetic and copies ran while one was open for 12% of the time, Pallas kernels for 0%

commit v1 on v0

--- a/solution.py
+++ b/solution.py
@@ -1,6 +1,7 @@
 import jax
 import jax.numpy as jnp
 from jax import lax
+from jax.sharding import Mesh
 from jax.sharding import PartitionSpec as P
 
 
@@ -23,6 +24,8 @@
 
 def on_device(route_ids, gate_values, out_grad, down_weight, hidden):
     experts = lax.axis_size("expert")
+    chips = lax.axis_size("z")
+    cores = lax.axis_size("core")
     capacity = hidden.shape[3]
     inner_width = hidden.shape[4]
     feature_width = out_grad.shape[1]
@@ -41,8 +44,18 @@
     )
     outgoing = jnp.dot(slot_map, scaled, preferred_element_type=jnp.float32)
     outgoing = outgoing.astype(jnp.bfloat16).reshape(experts, capacity, feature_width)
+    incoming = lax.all_to_all(outgoing, "expert", split_axis=0, concat_axis=0, tiled=True)
+    grad_rows = incoming.reshape(-1, feature_width)
+    block = inner_width // (chips * cores)
+    rows_perm = (
+        rows_in.reshape(-1, chips, cores, block).transpose(0, 2, 1, 3).reshape(-1, inner_width)
+    )
+    partial_term = jnp.einsum(
+        "sh,sd->hd", rows_perm, grad_rows, preferred_element_type=jnp.float32
+    )
+    half = lax.psum_scatter(partial_term, "core", scatter_dimension=0, tiled=True)
+    weight_grad = lax.psum_scatter(half, "z", scatter_dimension=0, tiled=True)
     returned = lax.all_to_all(expert_out, "expert", split_axis=0, concat_axis=0, tiled=True)
-    incoming = lax.all_to_all(outgoing, "expert", split_axis=0, concat_axis=0, tiled=True)
     gathered = jnp.einsum(
         "sr,sd->rd",
         slot_map,
@@ -52,28 +65,29 @@
     gathered = gathered.reshape(tok_rows, routes, feature_width)
     mixed_out = jnp.sum(gate_values[:, :, None] * gathered, axis=1).astype(jnp.bfloat16)
     gate_grad = jnp.sum(gathered * grads_f[:, None, :], axis=2)
-    grad_rows = incoming.reshape(-1, feature_width)
     hidden_grad = jnp.einsum("sd,hd->sh", grad_rows, weight_mat, preferred_element_type=jnp.float32)
     hidden_grad = hidden_grad.astype(jnp.bfloat16).reshape(hidden.shape)
-    partial_term = jnp.einsum("sh,sd->hd", rows_in, grad_rows, preferred_element_type=jnp.float32)
-    weight_grad = lax.psum_scatter(partial_term, "dp", scatter_dimension=0, tiled=True)
     return (mixed_out, gate_grad, hidden_grad, weight_grad[None])
 
 
 def solution(mesh):
+    n_dp = mesh.shape["dp"]
+    n_ex = mesh.shape["expert"]
+    sub = Mesh(mesh.devices.reshape(n_dp // 2, 2, n_ex), ("z", "core", "expert"))
+    tok = ("z", "core", "expert")
     in_specs = (
-        P(("dp", "expert"), None),
-        P(("dp", "expert"), None),
-        P(("dp", "expert"), None),
+        P(tok, None),
+        P(tok, None),
+        P(tok, None),
         P("expert", None, None),
-        P("dp", "expert", None, None, None),
+        P(("z", "core"), "expert", None, None, None),
     )
     out_specs = (
-        P(("dp", "expert"), None),
-        P(("dp", "expert"), None),
-        P("dp", "expert", None, None, None),
-        P("expert", "dp", None),
+        P(tok, None),
+        P(tok, None),
+        P(("z", "core"), "expert", None, None, None),
+        P("expert", ("z", "core"), None),
     )
     return jax.shard_map(
-        on_device, mesh=mesh, in_specs=in_specs, out_specs=out_specs, check_vma=False
+        on_device, mesh=sub, in_specs=in_specs, out_specs=out_specs, check_vma=False
     )

time: 240 us -> 223 us (0.929)
  waiting for transfers between devices: 137 us -> 103 us
  local copies, waits for them, and re-layouts: 42.5 us -> 55.4 us
  starting transfers between devices: 23.8 us -> 27.4 us
    unnamed x2 -> x3, waiting for transfers between devices: 64 us -> 7.57 us
    reduce_scatter x0 -> x1, waiting for transfers between devices: none -> 31.2 us  [on_device(): lax.psum_scatter(partial_term, 'core', scatter_dimension=0, tiled=True)]
    all_to_all x1, waiting for transfers between devices: 38.5 us -> 24.6 us  [on_device(): lax.all_to_all(outgoing, 'expert', split_axis=0, concat_axis=0, tiled=True)]
    another operation x0 -> x1, local copies, waits for them, and re-layouts: none -> 9.85 us  [on_device(): rows_in.reshape(-1, chips, cores, block).transpose(0, 2, 1, 3)]
    transpose x0 -> x1, local copies, waits for them, and re-layouts: none -> 6 us  [on_device(): rows_in.reshape(-1, chips, cores, block).transpose(0, 2, 1, 3)]
    all_to_all x1, waiting for transfers between devices: 34.7 us -> 39.8 us  [on_device(): lax.all_to_all(expert_out, 'expert', split_axis=0, concat_axis=0, tiled=T...]
    all_to_all x1, starting transfers between devices: 6.29 us -> 9.91 us  [on_device(): lax.all_to_all(expert_out, 'expert', split_axis=0, concat_axis=0, tiled=T...]
    unnamed x11, local copies, waits for them, and re-layouts: 17.1 us -> 14 us
  transfers between devices with their start and end apart: 3 -> 4, of which waited for: 3 -> 4; matrix products, arithmetic and copies ran while one was open for 12% -> 20% of each run, Pallas kernels for 0% -> 0%
where the time goes in v1:
time: 223 us; the launch traced here: 222 us
  waiting for transfers between devices  103 us (46%)
  local copies, waits for them, and re-layouts  55.4 us (25%)
  starting transfers between devices  27.4 us (12%)
  matrix products  19.5 us (9%)
  between operations  14.1 us (6%)
  other arithmetic  2.25 us (1%)
    all_to_all x1, waiting for transfers between devices, on_device(): lax.all_to_all(expert_out, 'expert', split_axis=0, concat_axis=0, tiled=T...  39.8 us
    reduce_scatter x1, waiting for transfers between devices, on_device(): lax.psum_scatter(partial_term, 'core', scatter_dimension=0, tiled=True)  31.2 us
    all_to_all x1, waiting for transfers between devices, on_device(): lax.all_to_all(outgoing, 'expert', split_axis=0, concat_axis=0, tiled=True)  24.6 us
    all_to_all x1, starting transfers between devices, on_device(): lax.all_to_all(outgoing, 'expert', split_axis=0, concat_axis=0, tiled=True)  17.4 us
    unnamed x11, local copies, waits for them, and re-layouts  14 us
    all_to_all x1, starting transfers between devices, on_device(): lax.all_to_all(expert_out, 'expert', split_axis=0, concat_axis=0, tiled=T...  9.91 us
    another operation x1, local copies, waits for them, and re-layouts, on_device(): rows_in.reshape(-1, chips, cores, block).transpose(0, 2, 1, 3)  9.85 us
    unnamed x3, waiting for transfers between devices  7.57 us
  transfers between devices with their start and end apart: 4, of which 4 were waited for; matrix products, arithmetic and copies ran while one was open for 20% of the time, Pallas kernels for 0%

profile of v1, /device:TPU:6, one launch (start us, length us, event | category | flops | bytes accessed | tf_op | source)
XLA Modules:
  0.0 221.9 jit_solution(12238875322582777462)
XLA Ops:
  9.4 3.4 %mul.50.clone = f32[128,2,2048]{2,1,0:T(2,128)} broadcast(bf16[128,2048]{1,0:T(8,128)(2,1)} %param.7), dimensions={0,2} | broadcast | bytes 2621440 | tf_op jit(solution)/shard_map/mul | solution.py:67
  12.8 3.7 %mul.54 = f32[256,2048]{1,0:T(8,128)} reshape(f32[128,2,2048]{2,1,0:T(2,128)} %mul.50.clone) | data formatting | bytes 4194304 | tf_op jit(solution)/shard_map/mul | solution.py:67
  16.5 3.2 %convolution_convert_fusion = bf16[320,2048]{1,0:T(8,128)(2,1)} fusion(f32[256,2048]{1,0:T(8,128)} %mul.54, f32[256]{0:T(256)S(1)} %mul.52, s32[256]{0:T(256)S(1)} %convert_add_fusion), kind=kOutput, calls=%fused_computation.6 | convolution fusion | flops 337330176 | bytes 3409920 | tf_op jit(solution)/shard_map/dot_general | solution.py:45
  19.7 3.3 %reshape.77 = bf16[32,10,2048]{2,1,0:T(8,128)(2,1)} reshape(bf16[320,2048]{1,0:T(8,128)(2,1)} %convolution_convert_fusion) | data formatting | bytes 2621440 | tf_op jit(solution)/shard_map/reshape | solution.py:46
  23.1 17.4 %all-to-all-start.1 = ((bf16[32,10,2048]{2,1,0:T(8,128)(2,1)}), bf16[32,10,2048]{2,1,0:T(8,128)(2,1)}, u32[]{:S(2)}, u32[]{:S(2)}) async-start(bf16[32,10,2048]{2,1,0:T(8,128)(2,1)} %reshape.77), calls=%async_computation.1 | async-start | bytes 4194304 | tf_op jit(solution)/shard_map/all_to_all | solution.py:47
  40.6 2.2 copy.21
  42.8 9.8 %reshape_reshape.3 = bf16[320,16,2,24]{3,2,1,0:T(2,128)(2,1)} reshape(bf16[1,1,32,10,768]{4,3,2,1,0:T(8,128)(2,1)} %copy.21) | data formatting | bytes 983040 | tf_op jit(solution)/shard_map/reshape;reshape | solution.py:51
  52.6 6.0 %copy.26 = bf16[320,2,16,24]{0,3,2,1:T(8,128)(2,1)} copy(bf16[320,2,16,24]{3,1,2,0:T(2,128)(2,1)} %bitcast.20) | data formatting | bytes 983040 | tf_op jit(solution)/shard_map/transpose | solution.py:51
  58.6 24.6 %all-to-all-done.1 = bf16[32,10,2048]{2,1,0:T(8,128)(2,1)} async-done(((bf16[32,10,2048]{2,1,0:T(8,128)(2,1)}), bf16[32,10,2048]{2,1,0:T(8,128)(2,1)}, u32[]{:S(2)}, u32[]{:S(2)}) %all-to-all-start.1) | async-done | bytes 1310752 | tf_op jit(solution)/shard_map/all_to_all | solution.py:47
  83.3 3.6 %reshape.78 = bf16[320,2048]{1,0:T(8,128)(2,1)} reshape(bf16[32,10,2048]{2,1,0:T(8,128)(2,1)} %all-to-all-done.1) | data formatting | bytes 2621440 | tf_op jit(solution)/shard_map/reshape | solution.py:48
  86.9 6.0 %convolution_bitcast_fusion = f32[768,2048]{0,1:T(8,128)} fusion(bf16[320,2048]{1,0:T(8,128)(2,1)} %reshape.78, bf16[320,768]{0,1:T(8,128)(2,1)} %bitcast.22), kind=kOutput, calls=%fused_computation | convolution fusion | flops 1006632960 | bytes 8093696 | tf_op jit(solution)/shard_map/sh,sd->hd/dot_general | solution.py:53
  92.9 31.2 %reduce-scatter.5.cloned.1.call-done = f32[384,2048]{0,1:T(8,128)} async-done(((f32[768,2048]{0,1:T(8,128)}), f32[384,2048]{0,1:T(8,128)}) %reduce-scatter.5.cloned.1.call-update) | async-done | bytes 3145744 | tf_op jit(solution)/shard_map/reduce_scatter | solution.py:56
  124.2 3.5 %copy.29 = f32[384,2048]{1,0:T(8,128)} copy(f32[384,2048]{0,1:T(8,128)} %reduce-scatter.5.cloned.1.call-done) | data formatting | bytes 6291456
  129.7 3.3 %fusion.4 = bf16[320,2048]{1,0:T(8,128)(2,1)} fusion(bf16[320,768]{1,0:T(8,128)(2,1)} %reshape.74, bf16[1,768,2048]{2,1,0:T(8,128)(2,1)S(1)} %copy-done), kind=kOutput, calls=%fused_computation.5 | convolution fusion | flops 1007288320 | bytes 4947968 | tf_op jit(solution)/shard_map/dot_general | solution.py:37
  133.0 3.4 %reshape.75 = bf16[32,10,2048]{2,1,0:T(8,128)(2,1)} reshape(bf16[320,2048]{1,0:T(8,128)(2,1)} %fusion.4) | data formatting | bytes 2621440 | tf_op jit(solution)/shard_map/reshape | solution.py:38
  136.4 9.9 %all-to-all-start = ((bf16[32,10,2048]{2,1,0:T(8,128)(2,1)}), bf16[32,10,2048]{2,1,0:T(8,128)(2,1)}, u32[]{:S(2)}, u32[]{:S(2)}) async-start(bf16[32,10,2048]{2,1,0:T(8,128)(2,1)} %reshape.75), calls=%async_computation | async-start | bytes 4194304 | tf_op jit(solution)/shard_map/all_to_all | solution.py:58
  146.3 2.1 convert_element_type.31
  148.7 3.3 %fusion.7 = bf16[320,768]{1,0:T(8,128)(2,1)} fusion(bf16[320,2048]{1,0:T(8,128)(2,1)} %reshape.78, bf16[1,768,2048]{2,1,0:T(8,128)(2,1)S(1)} %copy-done), kind=kOutput, calls=%fused_computation.10 | convolution fusion | flops 1006878720 | bytes 4947968 | tf_op jit(solution)/shard_map/sd,hd->sh/dot_general | solution.py:68
  156.2 39.8 %all-to-all-done = bf16[32,10,2048]{2,1,0:T(8,128)(2,1)} async-done(((bf16[32,10,2048]{2,1,0:T(8,128)(2,1)}), bf16[32,10,2048]{2,1,0:T(8,128)(2,1)}, u32[]{:S(2)}, u32[]{:S(2)}) %all-to-all-start) | async-done | bytes 1310752 | tf_op jit(solution)/shard_map/all_to_all | solution.py:58
  196.0 3.6 %reshape.81 = bf16[320,2048,1]{1,0,2:T(8,128)(2,1)} reshape(bf16[32,10,2048]{2,1,0:T(8,128)(2,1)} %all-to-all-done) | data formatting | bytes 2621440 | tf_op jit(solution)/shard_map/reshape | solution.py:62
  199.6 3.4 %multiply_reduce_fusion = (f32[128,2]{0,1:T(2,128)}, bf16[128,2048]{1,0:T(8,128)(2,1)}) fusion(f32[128,2048]{1,0:T(8,128)} %convert_element_type.31, f32[128,2]{0,1:T(2,128)S(1)} %copy-done.1, bf16[320,2048,1]{1,0,2:T(8,128)(2,1)} %reshape.81, pred[128,2,320]{2,1,0:T(4,128)(4,1)S(1)} %eq.47), kind=kOutput, calls=%fused_computation.8 | convolution fusion | flops 337379072 | bytes 2967552 | tf_op jit(solution)/shard_map/sr,sd->rd/dot_general | solution.py:59
  203.0 7.5 %reduce-scatter.7.cloned.1.call-done = f32[24,2048]{1,0:T(8,128)} async-done(((f32[384,2048]{1,0:T(8,128)}), f32[24,2048]{1,0:T(8,128)}) %reduce-scatter.7.cloned.1.call-update) | async-done | bytes 196624
  210.5 2.3 %copy.30 = f32[24,2048]{0,1:T(8,128)} copy(f32[24,2048]{1,0:T(8,128)} %reduce-scatter.7.cloned.1.call-done) | data formatting | bytes 393216
  212.8 2.2 copy.28
  (19 shorter events, 8.8 us)
Async XLA Ops:
  7.2 122.6 %copy-start = (bf16[1,768,2048]{2,1,0:T(8,128)(2,1)S(1)}, bf16[1,768,2048]{2,1,0:T(8,128)(2,1)}, u32[]{:S(2)}) copy-start(bf16[1,768,2048]{2,1,0:T(8,128)(2,1)} %param.8) | copy-start | bytes 9437188
  23.1 60.2 %all-to-all-start.1 = ((bf16[32,10,2048]{2,1,0:T(8,128)(2,1)}), bf16[32,10,2048]{2,1,0:T(8,128)(2,1)}, u32[]{:S(2)}, u32[]{:S(2)}) async-start(bf16[32,10,2048]{2,1,0:T(8,128)(2,1)} %reshape.77), calls=%async_computation.1 | async-start | bytes 4194304 | tf_op jit(solution)/shard_map/all_to_all | solution.py:47
  40.5 83.6 %reduce-scatter.5.cloned.1.call-start = ((), (), s32[]{:S(2)}) async-start(), calls=%async_computation.4 | async-start | bytes 9437184 | tf_op jit(solution)/shard_map/reduce_scatter | solution.py:56
  92.9 117.7 %reduce-scatter.7.cloned.1.call-start = ((), (), s32[]{:S(2)}) async-start(), calls=%async_computation.5 | async-start | bytes 3342336
  136.4 59.6 %all-to-all-start = ((bf16[32,10,2048]{2,1,0:T(8,128)(2,1)}), bf16[32,10,2048]{2,1,0:T(8,128)(2,1)}, u32[]{:S(2)}, u32[]{:S(2)}) async-start(bf16[32,10,2048]{2,1,0:T(8,128)(2,1)} %reshape.75), calls=%async_computation | async-start | bytes 4194304 | tf_op jit(solution)/shard_map/all_to_all | solution.py:58
  154.1 45.5 %copy-start.1 = (f32[128,2]{0,1:T(2,128)S(1)}, f32[128,2]{0,1:T(2,128)}, u32[]{:S(2)}) copy-start(f32[128,2]{0,1:T(2,128)} %param.6) | copy-start | bytes 3076
Sparse Core Ops, SparseCore 0:
  93.0 31.1 reduce-scatter.4
  127.8 82.6 reduce-scatter.6

commit v2 on v1

--- a/solution.py
+++ b/solution.py
@@ -20,6 +20,40 @@
     slot_index = flat_ids * capacity + slot_rank
     slots_all = jnp.arange(experts * capacity, dtype=jnp.int32)
     return (slots_all[:, None] == slot_index[None, :]).astype(jnp.bfloat16)
+
+
+def ring_reduce_scatter(blocks, axis, n):
+    d = lax.axis_index(axis)
+    down = [(i, (i - 1) % n) for i in range(n)]
+    up = [(i, (i + 1) % n) for i in range(n)]
+
+    def blk(j):
+        return lax.dynamic_index_in_dim(blocks, j % n, axis=0, keepdims=False)
+
+    n_a = n // 2
+    n_b = n - 1 - n_a
+    acc_a = None
+    acc_b = None
+    for t in range(n_a):
+        own = blk(d + n - n_a + t)
+        acc_a = lax.ppermute(own if acc_a is None else acc_a + own, axis, down)
+        if t < n_b:
+            own_b = blk(d + n_b - t)
+            acc_b = lax.ppermute(own_b if acc_b is None else acc_b + own_b, axis, up)
+    out = blk(d) + acc_a
+    if acc_b is not None:
+        out = out + acc_b
+    return out
+
+
+def reduce_over_dp(partial_term, chips, cores):
+    rows = partial_term.shape[0]
+    parts = partial_term.reshape(cores, chips, rows // (cores * chips), -1)
+    c = lax.axis_index("core")
+    keep = lax.dynamic_index_in_dim(parts, c, axis=0, keepdims=False)
+    give = lax.dynamic_index_in_dim(parts, 1 - c, axis=0, keepdims=False)
+    got = lax.ppermute(give, "core", [(0, 1), (1, 0)])
+    return ring_reduce_scatter(keep + got, "z", chips)
 
 
 def on_device(route_ids, gate_values, out_grad, down_weight, hidden):
@@ -53,8 +87,7 @@
     partial_term = jnp.einsum(
         "sh,sd->hd", rows_perm, grad_rows, preferred_element_type=jnp.float32
     )
-    half = lax.psum_scatter(partial_term, "core", scatter_dimension=0, tiled=True)
-    weight_grad = lax.psum_scatter(half, "z", scatter_dimension=0, tiled=True)
+    weight_grad = reduce_over_dp(partial_term, chips, cores)
     returned = lax.all_to_all(expert_out, "expert", split_axis=0, concat_axis=0, tiled=True)
     gathered = jnp.einsum(
         "sr,sd->rd",

time: 223 us -> 231 us (1.036)
  starting transfers between devices: 27.4 us -> 90.9 us
  waiting for transfers between devices: 103 us -> 49.2 us
  other arithmetic: 2.25 us -> 19.3 us
  between operations: 14.1 us -> 1.03 us
  local copies, waits for them, and re-layouts: 55.4 us -> 51.8 us
  matrix products: 19.5 us -> 16.8 us
    ppermute x0 -> x16, starting transfers between devices: none -> 67 us  [the longest x8 44.9 us: ring_reduce_scatter(): acc_a = lax.ppermute(own if acc_a is None else acc_a + own, axis, down)]
    all_to_all x1, waiting for transfers between devices: 39.8 us -> 0.01 us  [on_device(): lax.all_to_all(expert_out, 'expert', split_axis=0, concat_axis=0, tiled=T...]
    reduce_scatter x1 -> x0, waiting for transfers between devices: 31.2 us -> none  [on_device(): lax.psum_scatter(partial_term, 'core', scatter_dimension=0, tiled=True)]
    ppermute x0 -> x16, waiting for transfers between devices: none -> 24.5 us  [the longest x7 11.3 us: ring_reduce_scatter(): acc_b = lax.ppermute(own_b if acc_b is None else acc_b + own_b, axis, up)]
    add x0 -> x8, other arithmetic: none -> 15.3 us  [the longest x7 11.8 us: ring_reduce_scatter(): acc_a = lax.ppermute(own if acc_a is None else acc_a + own, axis, down)]
    unnamed x3 -> x0, waiting for transfers between devices: 7.57 us -> none
    unnamed x11 -> x12, local copies, waits for them, and re-layouts: 14 us -> 8.5 us
    all_to_all x1, starting transfers between devices: 9.91 us -> 6.39 us  [on_device(): lax.all_to_all(expert_out, 'expert', split_axis=0, concat_axis=0, tiled=T...]
  transfers between devices with their start and end apart: 4 -> 18, of which waited for: 4 -> 9; matrix products, arithmetic and copies ran while one was open for 20% -> 23% of each run, Pallas kernels for 0% -> 0%
where the time goes in v2:
time: 231 us; the launch traced here: 229 us
  starting transfers between devices  90.9 us (39%)
  local copies, waits for them, and re-layouts  51.8 us (22%)
  waiting for transfers between devices  49.2 us (21%)
  other arithmetic  19.3 us (8%)
  matrix products  16.8 us (7%)
    ppermute x8, starting transfers between devices, ring_reduce_scatter(): acc_a = lax.ppermute(own if acc_a is None else acc_a + own, axis, down)  44.9 us
    all_to_all x1, waiting for transfers between devices, on_device(): lax.all_to_all(outgoing, 'expert', split_axis=0, concat_axis=0, tiled=True)  24.6 us
    ppermute x7, starting transfers between devices, ring_reduce_scatter(): acc_b = lax.ppermute(own_b if acc_b is None else acc_b + own_b, axis, up)  20.2 us
    all_to_all x1, starting transfers between devices, on_device(): lax.all_to_all(outgoing, 'expert', split_axis=0, concat_axis=0, tiled=True)  17.5 us
    add x7, other arithmetic, ring_reduce_scatter(): acc_a = lax.ppermute(own if acc_a is None else acc_a + own, axis, down)  11.8 us
    ppermute x7, waiting for transfers between devices, ring_reduce_scatter(): acc_b = lax.ppermute(own_b if acc_b is None else acc_b + own_b, axis, up)  11.3 us
    another operation x1, local copies, waits for them, and re-layouts, on_device(): rows_in.reshape(-1, chips, cores, block).transpose(0, 2, 1, 3)  9.84 us
    unnamed x12, local copies, waits for them, and re-layouts  8.5 us
  transfers between devices with their start and end apart: 18, of which 9 were waited for; matrix products, arithmetic and copies ran while one was open for 23% of the time, Pallas kernels for 0%

profile of v2, /device:TPU:6, one launch (start us, length us, event | category | flops | bytes accessed | tf_op | source)
XLA Modules:
  0.0 229.0 jit_solution(7016908744397970629)
XLA Ops:
  1.9 3.4 %mul.50.clone = f32[128,2,2048]{2,1,0:T(2,128)} broadcast(bf16[128,2048]{1,0:T(8,128)(2,1)} %param.7), dimensions={0,2} | broadcast | bytes 2621440 | tf_op jit(solution)/shard_map/mul | solution.py:100
  5.3 3.7 %mul.54 = f32[256,2048]{1,0:T(8,128)} reshape(f32[128,2,2048]{2,1,0:T(2,128)} %mul.50.clone) | data formatting | bytes 4194304 | tf_op jit(solution)/shard_map/mul | solution.py:100
  12.5 3.3 %reshape.80 = bf16[32,10,2048]{2,1,0:T(8,128)(2,1)} reshape(bf16[320,2048]{1,0:T(8,128)(2,1)} %convolution_convert_fusion) | data formatting | bytes 2621440 | tf_op jit(solution)/shard_map/reshape | solution.py:80
  15.8 17.5 %all-to-all-start.1 = ((bf16[32,10,2048]{2,1,0:T(8,128)(2,1)}), bf16[32,10,2048]{2,1,0:T(8,128)(2,1)}, u32[]{:S(2)}, u32[]{:S(2)}) async-start(bf16[32,10,2048]{2,1,0:T(8,128)(2,1)} %reshape.80), calls=%async_computation.1 | async-start | bytes 4194304 | tf_op jit(solution)/shard_map/all_to_all | solution.py:81
  35.5 9.8 %reshape_reshape.3 = bf16[320,16,2,24]{3,2,1,0:T(2,128)(2,1)} reshape(bf16[1,1,32,10,768]{4,3,2,1,0:T(8,128)(2,1)} %copy.11) | data formatting | bytes 983040 | tf_op jit(solution)/shard_map/reshape;reshape | solution.py:85
  45.4 6.0 %copy.16 = bf16[320,2,16,24]{0,3,2,1:T(8,128)(2,1)} copy(bf16[320,2,16,24]{3,1,2,0:T(2,128)(2,1)} %bitcast.63) | data formatting | bytes 983040 | tf_op jit(solution)/shard_map/transpose | solution.py:85
  51.4 24.6 %all-to-all-done.1 = bf16[32,10,2048]{2,1,0:T(8,128)(2,1)} async-done(((bf16[32,10,2048]{2,1,0:T(8,128)(2,1)}), bf16[32,10,2048]{2,1,0:T(8,128)(2,1)}, u32[]{:S(2)}, u32[]{:S(2)}) %all-to-all-start.1) | async-done | bytes 1310752 | tf_op jit(solution)/shard_map/all_to_all | solution.py:81
  76.0 3.6 %reshape.81 = bf16[320,2048]{1,0:T(8,128)(2,1)} reshape(bf16[32,10,2048]{2,1,0:T(8,128)(2,1)} %all-to-all-done.1) | data formatting | bytes 2621440 | tf_op jit(solution)/shard_map/reshape | solution.py:82
  88.4 5.9 %collective-permute-done = f32[16,24,2048]{2,1,0:T(8,128)} collective-permute-done((f32[16,24,2048]{2,1,0:T(8,128)}, f32[16,24,2048]{2,1,0:T(8,128)}, u32[]{:S(2)}, u32[]{:S(2)}) %collective-permute-start) | collective-permute-done | bytes 3145760 | tf_op jit(solution)/shard_map/ppermute | solution.py:55
  94.4 3.5 %bitcast_add_fusion = f32[16,24,2048]{2,1,0:T(8,128)S(1)} fusion(f32[16,24,2048]{2,1,0:T(8,128)} %collective-permute-done, f32[2,16,24,2048]{3,2,1,0:T(8,128)} %bitcast.62, s32[]{:T(128)S(6)} %select_n.123), kind=kLoop, calls=%fused_computation | loop fusion | flops 786432 | bytes 9437188 | tf_op jit(solution)/shard_map/add | solution.py:56
  99.6 18.1 %collective-permute-start.1 = (f32[24,2048]{1,0:T(8,128)S(1)}, f32[24,2048]{1,0:T(8,128)}, u32[]{:S(2)}, u32[]{:S(2)}) collective-permute-start(f32[24,2048]{1,0:T(8,128)S(1)} %get-tuple-element.26), channel_id=1, source_target_pairs={{0,960},{64,0},{128,64},{192,128},{256,192},{320,256},{384,320},{4... | collective-permute-start | bytes 589832 | tf_op jit(solution)/shard_map/ppermute | solution.py:39
  123.2 5.7 %collective-permute-start.2 = (f32[24,2048]{1,0:T(8,128)S(1)}, f32[24,2048]{1,0:T(8,128)}, u32[]{:S(2)}, u32[]{:S(2)}) collective-permute-start(f32[24,2048]{1,0:T(8,128)S(1)} %bitcast_add_fusion.13), channel_id=1, source_target_pairs={{0,960},{64,0},{128,64},{192,128},{256,192},{320,256},{384,320},{4... | collective-permute-start | bytes 589832 | tf_op jit(solution)/shard_map/ppermute | solution.py:39
  134.4 5.7 %collective-permute-start.3 = (f32[24,2048]{1,0:T(8,128)}, f32[24,2048]{1,0:T(8,128)S(1)}, u32[]{:S(2)}, u32[]{:S(2)}) collective-permute-start(f32[24,2048]{1,0:T(8,128)} %get-tuple-element.24), channel_id=1, source_target_pairs={{0,960},{64,0},{128,64},{192,128},{256,192},{320,256},{384,320},{4... | collective-permute-start | bytes 589832 | tf_op jit(solution)/shard_map/ppermute | solution.py:39
  145.3 3.3 %reshape.78 = bf16[32,10,2048]{2,1,0:T(8,128)(2,1)} reshape(bf16[320,2048]{1,0:T(8,128)(2,1)} %fusion.4) | data formatting | bytes 2621440 | tf_op jit(solution)/shard_map/reshape | solution.py:72
  148.7 6.4 %all-to-all-start = ((bf16[32,10,2048]{2,1,0:T(8,128)(2,1)}), bf16[32,10,2048]{2,1,0:T(8,128)(2,1)}, u32[]{:S(2)}, u32[]{:S(2)}) async-start(bf16[32,10,2048]{2,1,0:T(8,128)(2,1)} %reshape.78), calls=%async_computation | async-start | bytes 4194304 | tf_op jit(solution)/shard_map/all_to_all | solution.py:91
  157.0 5.1 %collective-permute-start.4 = (f32[24,2048]{1,0:T(8,128)}, f32[24,2048]{1,0:T(8,128)S(1)}, u32[]{:S(2)}, u32[]{:S(2)}) collective-permute-start(f32[24,2048]{1,0:T(8,128)} %get-tuple-element.22), channel_id=1, source_target_pairs={{0,960},{64,0},{128,64},{192,128},{256,192},{320,256},{384,320},{4... | collective-permute-start | bytes 589832 | tf_op jit(solution)/shard_map/ppermute | solution.py:39
  165.6 5.4 %collective-permute-done.11 = f32[24,2048]{1,0:T(8,128)} collective-permute-done((f32[24,2048]{1,0:T(8,128)S(1)}, f32[24,2048]{1,0:T(8,128)}, u32[]{:S(2)}, u32[]{:S(2)}) %collective-permute-start.11) | collective-permute-done | bytes 196640 | tf_op jit(solution)/shard_map/ppermute | solution.py:42
  174.7 3.9 %collective-permute-start.12 = (f32[24,2048]{1,0:T(8,128)S(1)}, f32[24,2048]{1,0:T(8,128)}, u32[]{:S(2)}, u32[]{:S(2)}) collective-permute-start(f32[24,2048]{1,0:T(8,128)S(1)} %get-tuple-element.21), channel_id=1, source_target_pairs={{0,64},{64,128},{128,192},{192,256},{256,320},{320,384},{384,448},... | collective-permute-start | bytes 589832 | tf_op jit(solution)/shard_map/ppermute | solution.py:42
  187.4 3.9 %collective-permute-start.13 = (f32[24,2048]{1,0:T(8,128)}, f32[24,2048]{1,0:T(8,128)}, u32[]{:S(2)}, u32[]{:S(2)}) collective-permute-start(f32[24,2048]{1,0:T(8,128)} %get-tuple-element.19), channel_id=1, source_target_pairs={{0,64},{64,128},{128,192},{192,256},{256,320},{320,384},{384,448},... | collective-permute-start | bytes 589832 | tf_op jit(solution)/shard_map/ppermute | solution.py:42
  200.6 3.9 %collective-permute-start.14 = (f32[24,2048]{1,0:T(8,128)}, f32[24,2048]{1,0:T(8,128)}, u32[]{:S(2)}, u32[]{:S(2)}) collective-permute-start(f32[24,2048]{1,0:T(8,128)} %get-tuple-element.17), channel_id=1, source_target_pairs={{0,64},{64,128},{128,192},{192,256},{256,320},{320,384},{384,448},... | collective-permute-start | bytes 589832 | tf_op jit(solution)/shard_map/ppermute | solution.py:42
  204.5 3.3 %fusion.7 = bf16[320,768]{1,0:T(8,128)(2,1)} fusion(bf16[320,2048]{1,0:T(8,128)(2,1)} %reshape.81, bf16[1,768,2048]{2,1,0:T(8,128)(2,1)S(1)} %copy-done), kind=kOutput, calls=%fused_computation.11 | convolution fusion | flops 1006878720 | bytes 4947968 | tf_op jit(solution)/shard_map/sd,hd->sh/dot_general | solution.py:101
  212.0 3.6 %reshape.85 = bf16[320,2048,1]{1,0,2:T(8,128)(2,1)} reshape(bf16[32,10,2048]{2,1,0:T(8,128)(2,1)} %all-to-all-done) | data formatting | bytes 2621440 | tf_op jit(solution)/shard_map/reshape | solution.py:95
  219.6 4.3 %collective-permute-start.8 = (f32[24,2048]{1,0:T(8,128)S(1)}, f32[24,2048]{1,0:T(8,128)S(1)}, u32[]{:S(2)}, u32[]{:S(2)}) collective-permute-start(f32[24,2048]{1,0:T(8,128)S(1)} %get-tuple-element.14), channel_id=1, source_target_pairs={{0,960},{64,0},{128,64},{192,128},{256,192},{320,256},{384,320},{4... | collective-permute-start | bytes 589832 | tf_op jit(solution)/shard_map/ppermute | solution.py:39
  224.0 3.4 %multiply_reduce_fusion = (f32[128,2]{0,1:T(2,128)}, bf16[128,2048]{1,0:T(8,128)(2,1)}) fusion(f32[128,2048]{1,0:T(8,128)} %convert_element_type.31, f32[128,2]{0,1:T(2,128)S(1)} %copy-done.3, bf16[320,2048,1]{1,0,2:T(8,128)(2,1)} %reshape.85, pred[128,2,320]{2,1,0:T(4,128)(4,1)S(1)} %eq.64), kind=kOutput, calls=%fused_computation.9 | convolution fusion | flops 337379072 | bytes 2967552 | tf_op jit(solution)/shard_map/sr,sd->rd/dot_general | solution.py:92
  (57 shorter events, 70.5 us)
Async XLA Ops:
  0.6 141.4 %copy-start = (bf16[1,768,2048]{2,1,0:T(8,128)(2,1)S(1)}, bf16[1,768,2048]{2,1,0:T(8,128)(2,1)}, u32[]{:S(2)}) copy-start(bf16[1,768,2048]{2,1,0:T(8,128)(2,1)} %param.8) | copy-start | bytes 9437188
  5.3 3.7 %copy-start.3 = (f32[128,2]{0,1:T(2,128)S(1)}, f32[128,2]{0,1:T(2,128)}, u32[]{:S(2)}) copy-start(f32[128,2]{0,1:T(2,128)} %param.6) | copy-start | bytes 3076
  15.8 60.2 %all-to-all-start.1 = ((bf16[32,10,2048]{2,1,0:T(8,128)(2,1)}), bf16[32,10,2048]{2,1,0:T(8,128)(2,1)}, u32[]{:S(2)}, u32[]{:S(2)}) async-start(bf16[32,10,2048]{2,1,0:T(8,128)(2,1)} %reshape.80), calls=%async_computation.1 | async-start | bytes 4194304 | tf_op jit(solution)/shard_map/all_to_all | solution.py:81
  82.9 3.6 %copy-start.1 = (f32[2048,768]{0,1:T(8,128)}, f32[2048,768]{0,1:T(8,128)S(1)}, u32[]{:S(2)}) copy-start(f32[2048,768]{0,1:T(8,128)S(1)} %fusion.18) | copy-start | bytes 18874372
  86.5 7.9 %collective-permute-start = (f32[16,24,2048]{2,1,0:T(8,128)}, f32[16,24,2048]{2,1,0:T(8,128)}, u32[]{:S(2)}, u32[]{:S(2)}) collective-permute-start(f32[16,24,2048]{2,1,0:T(8,128)} %dynamic-slice_bitcast_fusion), channel_id=1, source_target_pairs={{0,32},{32,0},{1,33},{33,1},{2,34},{34,2},{3,35},{35,3},{4,36},{36... | collective-permute-start | bytes 9437192 | tf_op jit(solution)/shard_map/ppermute | solution.py:55
  97.9 1.6 copy-start.2
  99.6 22.6 %collective-permute-start.1 = (f32[24,2048]{1,0:T(8,128)S(1)}, f32[24,2048]{1,0:T(8,128)}, u32[]{:S(2)}, u32[]{:S(2)}) collective-permute-start(f32[24,2048]{1,0:T(8,128)S(1)} %get-tuple-element.26), channel_id=1, source_target_pairs={{0,960},{64,0},{128,64},{192,128},{256,192},{320,256},{384,320},{4... | collective-permute-start | bytes 589832 | tf_op jit(solution)/shard_map/ppermute | solution.py:39
  117.7 13.2 %collective-permute-start.9 = (f32[24,2048]{1,0:T(8,128)S(1)}, f32[24,2048]{1,0:T(8,128)}, u32[]{:S(2)}, u32[]{:S(2)}) collective-permute-start(f32[24,2048]{1,0:T(8,128)S(1)} %get-tuple-element.27), channel_id=1, source_target_pairs={{0,64},{64,128},{128,192},{192,256},{256,320},{320,384},{384,448},... | collective-permute-start | bytes 589832 | tf_op jit(solution)/shard_map/ppermute | solution.py:42
  123.2 9.3 %collective-permute-start.2 = (f32[24,2048]{1,0:T(8,128)S(1)}, f32[24,2048]{1,0:T(8,128)}, u32[]{:S(2)}, u32[]{:S(2)}) collective-permute-start(f32[24,2048]{1,0:T(8,128)S(1)} %bitcast_add_fusion.13), channel_id=1, source_target_pairs={{0,960},{64,0},{128,64},{192,128},{256,192},{320,256},{384,320},{4... | collective-permute-start | bytes 589832 | tf_op jit(solution)/shard_map/ppermute | solution.py:39
  134.4 20.7 %collective-permute-start.3 = (f32[24,2048]{1,0:T(8,128)}, f32[24,2048]{1,0:T(8,128)S(1)}, u32[]{:S(2)}, u32[]{:S(2)}) collective-permute-start(f32[24,2048]{1,0:T(8,128)} %get-tuple-element.24), channel_id=1, source_target_pairs={{0,960},{64,0},{128,64},{192,128},{256,192},{320,256},{384,320},{4... | collective-permute-start | bytes 589832 | tf_op jit(solution)/shard_map/ppermute | solution.py:39
  140.1 15.0 %collective-permute-start.10 = (f32[24,2048]{1,0:T(8,128)S(1)}, f32[24,2048]{1,0:T(8,128)}, u32[]{:S(2)}, u32[]{:S(2)}) collective-permute-start(f32[24,2048]{1,0:T(8,128)S(1)} %get-tuple-element.25), channel_id=1, source_target_pairs={{0,64},{64,128},{128,192},{192,256},{256,320},{320,384},{384,448},... | collective-permute-start | bytes 589832 | tf_op jit(solution)/shard_map/ppermute | solution.py:42
  148.7 63.4 %all-to-all-start = ((bf16[32,10,2048]{2,1,0:T(8,128)(2,1)}), bf16[32,10,2048]{2,1,0:T(8,128)(2,1)}, u32[]{:S(2)}, u32[]{:S(2)}) async-start(bf16[32,10,2048]{2,1,0:T(8,128)(2,1)} %reshape.78), calls=%async_computation | async-start | bytes 4194304 | tf_op jit(solution)/shard_map/all_to_all | solution.py:91
  157.0 8.6 %collective-permute-start.4 = (f32[24,2048]{1,0:T(8,128)}, f32[24,2048]{1,0:T(8,128)S(1)}, u32[]{:S(2)}, u32[]{:S(2)}) collective-permute-start(f32[24,2048]{1,0:T(8,128)} %get-tuple-element.22), channel_id=1, source_target_pairs={{0,960},{64,0},{128,64},{192,128},{256,192},{320,256},{384,320},{4... | collective-permute-start | bytes 589832 | tf_op jit(solution)/shard_map/ppermute | solution.py:39
  162.1 8.9 %collective-permute-start.11 = (f32[24,2048]{1,0:T(8,128)S(1)}, f32[24,2048]{1,0:T(8,128)}, u32[]{:S(2)}, u32[]{:S(2)}) collective-permute-start(f32[24,2048]{1,0:T(8,128)S(1)} %get-tuple-element.23), channel_id=1, source_target_pairs={{0,64},{64,128},{128,192},{192,256},{256,320},{320,384},{384,448},... | collective-permute-start | bytes 589832 | tf_op jit(solution)/shard_map/ppermute | solution.py:42
  172.8 8.1 %collective-permute-start.5 = (f32[24,2048]{1,0:T(8,128)}, f32[24,2048]{1,0:T(8,128)S(1)}, u32[]{:S(2)}, u32[]{:S(2)}) collective-permute-start(f32[24,2048]{1,0:T(8,128)} %get-tuple-element.20), channel_id=1, source_target_pairs={{0,960},{64,0},{128,64},{192,128},{256,192},{320,256},{384,320},{4... | collective-permute-start | bytes 589832 | tf_op jit(solution)/shard_map/ppermute | solution.py:39
  174.7 8.9 %collective-permute-start.12 = (f32[24,2048]{1,0:T(8,128)S(1)}, f32[24,2048]{1,0:T(8,128)}, u32[]{:S(2)}, u32[]{:S(2)}) collective-permute-start(f32[24,2048]{1,0:T(8,128)S(1)} %get-tuple-element.21), channel_id=1, source_target_pairs={{0,64},{64,128},{128,192},{192,256},{256,320},{320,384},{384,448},... | collective-permute-start | bytes 589832 | tf_op jit(solution)/shard_map/ppermute | solution.py:42
  185.5 7.9 %collective-permute-start.6 = (f32[24,2048]{1,0:T(8,128)}, f32[24,2048]{1,0:T(8,128)}, u32[]{:S(2)}, u32[]{:S(2)}) collective-permute-start(f32[24,2048]{1,0:T(8,128)} %get-tuple-element.18), channel_id=1, source_target_pairs={{0,960},{64,0},{128,64},{192,128},{256,192},{320,256},{384,320},{4... | collective-permute-start | bytes 589832 | tf_op jit(solution)/shard_map/ppermute | solution.py:39
  187.4 9.1 %collective-permute-start.13 = (f32[24,2048]{1,0:T(8,128)}, f32[24,2048]{1,0:T(8,128)}, u32[]{:S(2)}, u32[]{:S(2)}) collective-permute-start(f32[24,2048]{1,0:T(8,128)} %get-tuple-element.19), channel_id=1, source_target_pairs={{0,64},{64,128},{128,192},{192,256},{256,320},{320,384},{384,448},... | collective-permute-start | bytes 589832 | tf_op jit(solution)/shard_map/ppermute | solution.py:42
  198.5 17.1 %collective-permute-start.7 = (f32[24,2048]{1,0:T(8,128)}, f32[24,2048]{1,0:T(8,128)}, u32[]{:S(2)}, u32[]{:S(2)}) collective-permute-start(f32[24,2048]{1,0:T(8,128)} %get-tuple-element.16), channel_id=1, source_target_pairs={{0,960},{64,0},{128,64},{192,128},{256,192},{320,256},{384,320},{4... | collective-permute-start | bytes 589832 | tf_op jit(solution)/shard_map/ppermute | solution.py:39
  200.6 15.0 %collective-permute-start.14 = (f32[24,2048]{1,0:T(8,128)}, f32[24,2048]{1,0:T(8,128)}, u32[]{:S(2)}, u32[]{:S(2)}) collective-permute-start(f32[24,2048]{1,0:T(8,128)} %get-tuple-element.17), channel_id=1, source_target_pairs={{0,64},{64,128},{128,192},{192,256},{256,320},{320,384},{384,448},... | collective-permute-start | bytes 589832 | tf_op jit(solution)/shard_map/ppermute | solution.py:42
  216.9 10.5 %collective-permute-start.15 = (f32[24,2048]{1,0:T(8,128)S(1)}, f32[24,2048]{1,0:T(8,128)S(1)}, u32[]{:S(2)}, u32[]{:S(2)}) collective-permute-start(f32[24,2048]{1,0:T(8,128)S(1)} %get-tuple-element.15), channel_id=1, source_target_pairs={{0,64},{64,128},{128,192},{192,256},{256,320},{320,384},{384,448},... | collective-permute-start | bytes 589832 | tf_op jit(solution)/shard_map/ppermute | solution.py:42
  219.6 7.8 %collective-permute-start.8 = (f32[24,2048]{1,0:T(8,128)S(1)}, f32[24,2048]{1,0:T(8,128)S(1)}, u32[]{:S(2)}, u32[]{:S(2)}) collective-permute-start(f32[24,2048]{1,0:T(8,128)S(1)} %get-tuple-element.14), channel_id=1, source_target_pairs={{0,960},{64,0},{128,64},{192,128},{256,192},{320,256},{384,320},{4... | collective-permute-start | bytes 589832 | tf_op jit(solution)/shard_map/ppermute | solution.py:39

commit v3 on v1

--- a/solution.py
+++ b/solution.py
@@ -20,6 +20,17 @@
     slot_index = flat_ids * capacity + slot_rank
     slots_all = jnp.arange(experts * capacity, dtype=jnp.int32)
     return (slots_all[:, None] == slot_index[None, :]).astype(jnp.bfloat16)
+
+
+def reduce_over_dp(partial_term, chips, cores):
+    rows = partial_term.shape[0]
+    parts = partial_term.reshape(cores, chips, rows // (cores * chips), -1)
+    c = lax.axis_index("core")
+    keep = lax.dynamic_index_in_dim(parts, c, axis=0, keepdims=False)
+    give = lax.dynamic_index_in_dim(parts, 1 - c, axis=0, keepdims=False)
+    got = lax.ppermute(give, "core", [(0, 1), (1, 0)])
+    chip_sum = (keep + got).reshape(rows // cores, -1)
+    return lax.psum_scatter(chip_sum, "z", scatter_dimension=0, tiled=True)
 
 
 def on_device(route_ids, gate_values, out_grad, down_weight, hidden):
@@ -53,8 +64,7 @@
     partial_term = jnp.einsum(
         "sh,sd->hd", rows_perm, grad_rows, preferred_element_type=jnp.float32
     )
-    half = lax.psum_scatter(partial_term, "core", scatter_dimension=0, tiled=True)
-    weight_grad = lax.psum_scatter(half, "z", scatter_dimension=0, tiled=True)
+    weight_grad = reduce_over_dp(partial_term, chips, cores)
     returned = lax.all_to_all(expert_out, "expert", split_axis=0, concat_axis=0, tiled=True)
     gathered = jnp.einsum(
         "sr,sd->rd",

time: 223 us -> 200 us (0.90)
  waiting for transfers between devices: 103 us -> 83.9 us
  other arithmetic: 2.25 us -> 7.47 us
  local copies, waits for them, and re-layouts: 55.4 us -> 51.1 us
  matrix products: 19.5 us -> 16.8 us
    reduce_scatter x1, waiting for transfers between devices: 31.2 us -> 13.5 us  [reduce_over_dp(): return lax.psum_scatter(chip_sum, 'z', scatter_dimension=0, tiled=True)]
    unnamed x3 -> x1, waiting for transfers between devices: 7.57 us -> 0.02 us
    unnamed x11 -> x10, local copies, waits for them, and re-layouts: 14 us -> 7.68 us
    ppermute x0 -> x1, waiting for transfers between devices: none -> 5.97 us  [reduce_over_dp(): got = lax.ppermute(give, 'core', [(0, 1), (1, 0)])]
    add x0 -> x1, other arithmetic: none -> 5.23 us  [reduce_over_dp(): chip_sum = (keep + got).reshape(rows // cores, -1)]
    all_to_all x1, starting transfers between devices: 9.91 us -> 6.3 us  [on_device(): lax.all_to_all(expert_out, 'expert', split_axis=0, concat_axis=0, tiled=T...]
    dot_general x1, matrix products: 5.96 us -> 3.29 us  [on_device(): jnp.einsum('sh,sd->hd', rows_perm, grad_rows, preferred_element_type=jnp....]
  transfers between devices with their start and end apart: 4 -> 4, of which waited for: 4 -> 4; matrix products, arithmetic and copies ran while one was open for 20% -> 22% of each run, Pallas kernels for 0% -> 0%
where the time goes in v3:
time: 200 us; the launch traced here: 199 us
  waiting for transfers between devices  83.9 us (42%)
  local copies, waits for them, and re-layouts  51.1 us (26%)
  starting transfers between devices  25.7 us (13%)
  matrix products  16.8 us (8%)
  between operations  14.1 us (7%)
  other arithmetic  7.47 us (4%)
    all_to_all x1, waiting for transfers between devices, on_device(): lax.all_to_all(expert_out, 'expert', split_axis=0, concat_axis=0, tiled=T...  39.8 us
    all_to_all x1, waiting for transfers between devices, on_device(): lax.all_to_all(outgoing, 'expert', split_axis=0, concat_axis=0, tiled=True)  24.6 us
    all_to_all x1, starting transfers between devices, on_device(): lax.all_to_all(outgoing, 'expert', split_axis=0, concat_axis=0, tiled=True)  17.5 us
    reduce_scatter x1, waiting for transfers between devices, reduce_over_dp(): return lax.psum_scatter(chip_sum, 'z', scatter_dimension=0, tiled=True)  13.5 us
    another operation x1, local copies, waits for them, and re-layouts, on_device(): rows_in.reshape(-1, chips, cores, block).transpose(0, 2, 1, 3)  9.86 us
    unnamed x10, local copies, waits for them, and re-layouts  7.68 us
    mul x2, local copies, waits for them, and re-layouts, on_device(): gate_grad = jnp.sum(gathered * grads_f[:, None, :], axis=2)  7.11 us
    all_to_all x1, starting transfers between devices, on_device(): lax.all_to_all(expert_out, 'expert', split_axis=0, concat_axis=0, tiled=T...  6.3 us
  transfers between devices with their start and end apart: 4, of which 4 were waited for; matrix products, arithmetic and copies ran while one was open for 22% of the time, Pallas kernels for 0%

profile of v3, /device:TPU:6, one launch (start us, length us, event | category | flops | bytes accessed | tf_op | source)
XLA Modules:
  0.0 199.1 jit_solution(81606809067167617)
XLA Ops:
  9.4 3.4 %mul.50.clone = f32[128,2,2048]{2,1,0:T(2,128)} broadcast(bf16[128,2048]{1,0:T(8,128)(2,1)} %param.7), dimensions={0,2} | broadcast | bytes 2621440 | tf_op jit(solution)/shard_map/mul | solution.py:77
  12.8 3.7 %mul.54 = f32[256,2048]{1,0:T(8,128)} reshape(f32[128,2,2048]{2,1,0:T(2,128)} %mul.50.clone) | data formatting | bytes 4194304 | tf_op jit(solution)/shard_map/mul | solution.py:77
  16.5 3.3 %convolution_convert_fusion = bf16[320,2048]{1,0:T(8,128)(2,1)} fusion(f32[256,2048]{1,0:T(8,128)} %mul.54, f32[256]{0:T(256)S(1)} %mul.52, s32[256]{0:T(256)S(1)} %convert_add_fusion), kind=kOutput, calls=%fused_computation.7 | convolution fusion | flops 337330176 | bytes 3409920 | tf_op jit(solution)/shard_map/dot_general | solution.py:56
  19.8 3.3 %reshape.83 = bf16[32,10,2048]{2,1,0:T(8,128)(2,1)} reshape(bf16[320,2048]{1,0:T(8,128)(2,1)} %convolution_convert_fusion) | data formatting | bytes 2621440 | tf_op jit(solution)/shard_map/reshape | solution.py:57
  23.1 17.5 %all-to-all-start.1 = ((bf16[32,10,2048]{2,1,0:T(8,128)(2,1)}), bf16[32,10,2048]{2,1,0:T(8,128)(2,1)}, u32[]{:S(2)}, u32[]{:S(2)}) async-start(bf16[32,10,2048]{2,1,0:T(8,128)(2,1)} %reshape.83), calls=%async_computation.1 | async-start | bytes 4194304 | tf_op jit(solution)/shard_map/all_to_all | solution.py:58
  40.6 2.2 %copy.11 = bf16[1,1,32,10,768]{4,3,2,1,0:T(8,128)(2,1)} copy(bf16[1,1,32,10,768]{4,2,3,1,0:T(8,128)(2,1)} %param.9) | data formatting | bytes 983040 | tf_op args[4]
  42.8 9.9 %reshape_reshape.3 = bf16[320,16,2,24]{3,2,1,0:T(2,128)(2,1)} reshape(bf16[1,1,32,10,768]{4,3,2,1,0:T(8,128)(2,1)} %copy.11) | data formatting | bytes 983040 | tf_op jit(solution)/shard_map/reshape;reshape | solution.py:62
  52.7 6.0 %copy.16 = bf16[320,2,16,24]{0,3,2,1:T(8,128)(2,1)} copy(bf16[320,2,16,24]{3,1,2,0:T(2,128)(2,1)} %bitcast.28) | data formatting | bytes 983040 | tf_op jit(solution)/shard_map/transpose | solution.py:62
  58.7 24.6 %all-to-all-done.1 = bf16[32,10,2048]{2,1,0:T(8,128)(2,1)} async-done(((bf16[32,10,2048]{2,1,0:T(8,128)(2,1)}), bf16[32,10,2048]{2,1,0:T(8,128)(2,1)}, u32[]{:S(2)}, u32[]{:S(2)}) %all-to-all-start.1) | async-done | bytes 1310752 | tf_op jit(solution)/shard_map/all_to_all | solution.py:58
  83.3 3.6 %reshape.84 = bf16[320,2048]{1,0:T(8,128)(2,1)} reshape(bf16[32,10,2048]{2,1,0:T(8,128)(2,1)} %all-to-all-done.1) | data formatting | bytes 2621440 | tf_op jit(solution)/shard_map/reshape | solution.py:59
  86.8 3.3 %fusion.16 = f32[2048,768]{0,1:T(8,128)S(1)} fusion(bf16[320,768]{0,1:T(8,128)(2,1)} %bitcast.29, bf16[320,2048]{1,0:T(8,128)(2,1)} %reshape.84), kind=kOutput, calls=%fused_computation.24 | convolution fusion | flops 1006632960 | bytes 8093696 | tf_op jit(solution)/shard_map/sh,sd->hd/dot_general | solution.py:64
  95.7 6.0 %collective-permute-done = f32[16,24,2048]{2,1,0:T(8,128)} collective-permute-done((f32[16,24,2048]{2,1,0:T(8,128)}, f32[16,24,2048]{2,1,0:T(8,128)}, u32[]{:S(2)}, u32[]{:S(2)}) %collective-permute-start) | collective-permute-done | bytes 3145760 | tf_op jit(solution)/shard_map/ppermute | solution.py:31
  101.7 5.2 %bitcast_add_fusion = f32[16,24,2048]{2,1,0:T(8,128)} fusion(f32[16,24,2048]{2,1,0:T(8,128)} %collective-permute-done, f32[2,16,24,2048]{3,2,1,0:T(8,128)} %bitcast.26, s32[]{:T(128)S(6)} %select_n.7), kind=kLoop, calls=%fused_computation | loop fusion | flops 786432 | bytes 9437188 | tf_op jit(solution)/shard_map/add | solution.py:32
  109.0 3.3 %fusion.4 = bf16[320,2048]{1,0:T(8,128)(2,1)} fusion(bf16[320,768]{1,0:T(8,128)(2,1)} %reshape.80, bf16[1,768,2048]{2,1,0:T(8,128)(2,1)S(1)} %copy-done), kind=kOutput, calls=%fused_computation.6 | convolution fusion | flops 1007288320 | bytes 4947968 | tf_op jit(solution)/shard_map/dot_general | solution.py:48
  112.3 3.3 %reshape.81 = bf16[32,10,2048]{2,1,0:T(8,128)(2,1)} reshape(bf16[320,2048]{1,0:T(8,128)(2,1)} %fusion.4) | data formatting | bytes 2621440 | tf_op jit(solution)/shard_map/reshape | solution.py:49
  115.6 6.3 %all-to-all-start = ((bf16[32,10,2048]{2,1,0:T(8,128)(2,1)}), bf16[32,10,2048]{2,1,0:T(8,128)(2,1)}, u32[]{:S(2)}, u32[]{:S(2)}) async-start(bf16[32,10,2048]{2,1,0:T(8,128)(2,1)} %reshape.81), calls=%async_computation | async-start | bytes 4194304 | tf_op jit(solution)/shard_map/all_to_all | solution.py:68
  121.9 2.1 %convert_element_type.31 = f32[128,2048]{1,0:T(8,128)} convert(bf16[128,2048]{1,0:T(8,128)(2,1)} %param.7) | non-fusion elementwise | flops 262144 | bytes 1572864 | tf_op jit(solution)/shard_map/convert_element_type | solution.py:50
  124.3 3.3 %fusion.7 = bf16[320,768]{1,0:T(8,128)(2,1)} fusion(bf16[320,2048]{1,0:T(8,128)(2,1)} %reshape.84, bf16[1,768,2048]{2,1,0:T(8,128)(2,1)S(1)} %copy-done), kind=kOutput, calls=%fused_computation.11 | convolution fusion | flops 1006878720 | bytes 4947968 | tf_op jit(solution)/shard_map/sd,hd->sh/dot_general | solution.py:78
  127.6 2.1 %reshape.85 = bf16[1,1,32,10,768]{4,3,2,1,0:T(8,128)(2,1)} reshape(bf16[320,768]{1,0:T(8,128)(2,1)} %fusion.7) | data formatting | bytes 983040 | tf_op jit(solution)/shard_map/reshape | solution.py:79
  129.7 2.1 %copy.17 = bf16[1,1,32,10,768]{4,2,3,1,0:T(8,128)(2,1)} copy(bf16[1,1,32,10,768]{4,3,2,1,0:T(8,128)(2,1)} %reshape.85) | data formatting | bytes 983040
  131.8 39.8 %all-to-all-done = bf16[32,10,2048]{2,1,0:T(8,128)(2,1)} async-done(((bf16[32,10,2048]{2,1,0:T(8,128)(2,1)}), bf16[32,10,2048]{2,1,0:T(8,128)(2,1)}, u32[]{:S(2)}, u32[]{:S(2)}) %all-to-all-start) | async-done | bytes 1310752 | tf_op jit(solution)/shard_map/all_to_all | solution.py:68
  171.6 3.6 %reshape.89 = bf16[320,2048,1]{1,0,2:T(8,128)(2,1)} reshape(bf16[32,10,2048]{2,1,0:T(8,128)(2,1)} %all-to-all-done) | data formatting | bytes 2621440 | tf_op jit(solution)/shard_map/reshape | solution.py:72
  175.2 3.4 %multiply_reduce_fusion = (f32[128,2]{0,1:T(2,128)}, bf16[128,2048]{1,0:T(8,128)(2,1)}) fusion(f32[128,2048]{1,0:T(8,128)} %convert_element_type.31, f32[128,2]{0,1:T(2,128)S(1)} %copy-done.2, bf16[320,2048,1]{1,0,2:T(8,128)(2,1)} %reshape.89, pred[128,2,320]{2,1,0:T(4,128)(4,1)S(1)} %eq.47), kind=kOutput, calls=%fused_computation.9 | convolution fusion | flops 337379072 | bytes 2967552 | tf_op jit(solution)/shard_map/sr,sd->rd/dot_general | solution.py:69
  178.7 13.5 %reduce-scatter.2.cloned.1.call-done = f32[24,2048]{1,0:T(8,128)} async-done(((f32[384,2048]{1,0:T(8,128)}), f32[24,2048]{1,0:T(8,128)}) %reduce-scatter.2.cloned.1.call-update) | async-done | bytes 196624 | tf_op jit(solution)/shard_map/reduce_scatter | solution.py:33
  (19 shorter events, 10.1 us)
Async XLA Ops:
  7.2 101.8 %copy-start = (bf16[1,768,2048]{2,1,0:T(8,128)(2,1)S(1)}, bf16[1,768,2048]{2,1,0:T(8,128)(2,1)}, u32[]{:S(2)}) copy-start(bf16[1,768,2048]{2,1,0:T(8,128)(2,1)} %param.8) | copy-start | bytes 9437188
  23.1 60.2 %all-to-all-start.1 = ((bf16[32,10,2048]{2,1,0:T(8,128)(2,1)}), bf16[32,10,2048]{2,1,0:T(8,128)(2,1)}, u32[]{:S(2)}, u32[]{:S(2)}) async-start(bf16[32,10,2048]{2,1,0:T(8,128)(2,1)} %reshape.83), calls=%async_computation.1 | async-start | bytes 4194304 | tf_op jit(solution)/shard_map/all_to_all | solution.py:58
  40.6 151.7 %reduce-scatter.2.cloned.1.call-start = ((), (), s32[]{:S(2)}) async-start(), calls=%async_computation.3 | async-start | bytes 3342336 | tf_op jit(solution)/shard_map/reduce_scatter | solution.py:33
  90.1 3.7 %copy-start.1 = (f32[2048,768]{0,1:T(8,128)}, f32[2048,768]{0,1:T(8,128)S(1)}, u32[]{:S(2)}) copy-start(f32[2048,768]{0,1:T(8,128)S(1)} %fusion.16) | copy-start | bytes 18874372
  93.8 7.9 %collective-permute-start = (f32[16,24,2048]{2,1,0:T(8,128)}, f32[16,24,2048]{2,1,0:T(8,128)}, u32[]{:S(2)}, u32[]{:S(2)}) collective-permute-start(f32[16,24,2048]{2,1,0:T(8,128)} %dynamic-slice_bitcast_fusion), channel_id=1, source_target_pairs={{0,32},{32,0},{1,33},{33,1},{2,34},{34,2},{3,35},{35,3},{4,36},{36... | collective-permute-start | bytes 9437192 | tf_op jit(solution)/shard_map/ppermute | solution.py:31
  115.6 56.0 %all-to-all-start = ((bf16[32,10,2048]{2,1,0:T(8,128)(2,1)}), bf16[32,10,2048]{2,1,0:T(8,128)(2,1)}, u32[]{:S(2)}, u32[]{:S(2)}) async-start(bf16[32,10,2048]{2,1,0:T(8,128)(2,1)} %reshape.81), calls=%async_computation | async-start | bytes 4194304 | tf_op jit(solution)/shard_map/all_to_all | solution.py:68
  129.7 45.6 %copy-start.2 = (f32[128,2]{0,1:T(2,128)S(1)}, f32[128,2]{0,1:T(2,128)}, u32[]{:S(2)}) copy-start(f32[128,2]{0,1:T(2,128)} %param.6) | copy-start | bytes 3076
Sparse Core Ops, SparseCore 0:
  107.1 85.1 reduce-scatter.1

commit v4 on v1

--- a/solution.py
+++ b/solution.py
@@ -44,17 +44,29 @@
     )
     outgoing = jnp.dot(slot_map, scaled, preferred_element_type=jnp.float32)
     outgoing = outgoing.astype(jnp.bfloat16).reshape(experts, capacity, feature_width)
-    incoming = lax.all_to_all(outgoing, "expert", split_axis=0, concat_axis=0, tiled=True)
-    grad_rows = incoming.reshape(-1, feature_width)
     block = inner_width // (chips * cores)
-    rows_perm = (
-        rows_in.reshape(-1, chips, cores, block).transpose(0, 2, 1, 3).reshape(-1, inner_width)
-    )
-    partial_term = jnp.einsum(
-        "sh,sd->hd", rows_perm, grad_rows, preferred_element_type=jnp.float32
-    )
-    half = lax.psum_scatter(partial_term, "core", scatter_dimension=0, tiled=True)
-    weight_grad = lax.psum_scatter(half, "z", scatter_dimension=0, tiled=True)
+    c = lax.axis_index("core")
+    swap = [(0, 1), (1, 0)]
+    cols = rows_in.reshape(-1, chips, cores, block)
+    mine_cols = lax.dynamic_index_in_dim(cols, c, axis=2, keepdims=False)
+    give_cols = lax.dynamic_index_in_dim(cols, 1 - c, axis=2, keepdims=False)
+    got_cols = lax.ppermute(give_cols, "core", swap)
+    both_cols = jnp.concatenate([mine_cols, got_cols], axis=0).reshape(-1, chips * block)
+    n_split = 2
+    width = feature_width // n_split
+    grad_parts = []
+    weight_parts = []
+    for k in range(n_split):
+        piece = outgoing[:, :, k * width : (k + 1) * width]
+        got = lax.all_to_all(piece, "expert", split_axis=0, concat_axis=0, tiled=True)
+        got = got.reshape(-1, width)
+        grad_parts.append(got)
+        partner = lax.ppermute(got, "core", swap)
+        both = jnp.concatenate([got, partner], axis=0)
+        chip_part = jnp.einsum("sh,sd->hd", both_cols, both, preferred_element_type=jnp.float32)
+        weight_parts.append(lax.psum_scatter(chip_part, "z", scatter_dimension=0, tiled=True))
+    weight_grad = jnp.concatenate(weight_parts, axis=1)
+    grad_rows = jnp.concatenate(grad_parts, axis=1)
     returned = lax.all_to_all(expert_out, "expert", split_axis=0, concat_axis=0, tiled=True)
     gathered = jnp.einsum(
         "sr,sd->rd",

time: 223 us -> 261 us (1.17)
  blocking collectives: 0 us -> 33.9 us
  waiting for transfers between devices: 103 us -> 92.9 us
  local copies, waits for them, and re-layouts: 55.4 us -> 65.2 us
    all_to_all x0 -> x1, blocking collectives: none -> 33.9 us  [on_device(): lax.all_to_all(piece, 'expert', split_axis=0, concat_axis=0, tiled=True)]
    dynamic_slice x0 -> x3, local copies, waits for them, and re-layouts: none -> 20.7 us  [the longest x2 14.9 us: on_device(): mine_cols = lax.dynamic_index_in_dim(cols, c, axis=2, keepdims=False)]
    all_to_all x1, waiting for transfers between devices: 24.6 us -> 8.86 us  [on_device(): lax.all_to_all(piece, 'expert', split_axis=0, concat_axis=0, tiled=True)]
    reduce_scatter x1 -> x2, waiting for transfers between devices: 31.2 us -> 43.8 us  [on_device(): lax.psum_scatter(chip_part, 'z', scatter_dimension=0, tiled=True)]
    unnamed x11 -> x8, local copies, waits for them, and re-layouts: 14 us -> 5.37 us
    unnamed x3 -> x2, waiting for transfers between devices: 7.57 us -> 0.03 us
    ppermute x0 -> x3, starting transfers between devices: none -> 6.4 us  [the longest x2 4 us: on_device(): partner = lax.ppermute(got, 'core', swap)]
    transpose x1 -> x0, local copies, waits for them, and re-layouts: 6 us -> none  [on_device(): rows_in.reshape(-1, chips, cores, block).transpose(0, 2, 1, 3)]
  transfers between devices with their start and end apart: 4 -> 7, of which waited for: 4 -> 4; matrix products, arithmetic and copies ran while one was open for 20% -> 25% of each run, Pallas kernels for 0% -> 0%
where the time goes in v4:
time: 261 us; the launch traced here: 260 us
  waiting for transfers between devices  92.9 us (36%)
  local copies, waits for them, and re-layouts  65.2 us (25%)
  blocking collectives  33.9 us (13%)
  starting transfers between devices  29.5 us (11%)
  matrix products  20.2 us (8%)
  between operations  14.2 us (5%)
  other arithmetic  3.9 us (1%)
    reduce_scatter x2, waiting for transfers between devices, on_device(): lax.psum_scatter(chip_part, 'z', scatter_dimension=0, tiled=True)  43.8 us
    all_to_all x1, waiting for transfers between devices, on_device(): lax.all_to_all(expert_out, 'expert', split_axis=0, concat_axis=0, tiled=T...  39.9 us
    all_to_all x1, blocking collectives, on_device(): lax.all_to_all(piece, 'expert', split_axis=0, concat_axis=0, tiled=True)  33.9 us
    all_to_all x1, starting transfers between devices, on_device(): lax.all_to_all(piece, 'expert', split_axis=0, concat_axis=0, tiled=True)  17.3 us
    dynamic_slice x2, local copies, waits for them, and re-layouts, on_device(): mine_cols = lax.dynamic_index_in_dim(cols, c, axis=2, keepdims=False)  14.9 us
    another operation x1, local copies, waits for them, and re-layouts, on_device(): cols = rows_in.reshape(-1, chips, cores, block)  9.85 us
    all_to_all x1, waiting for transfers between devices, on_device(): lax.all_to_all(piece, 'expert', split_axis=0, concat_axis=0, tiled=True)  8.86 us
    mul x2, local copies, waits for them, and re-layouts, on_device(): gate_grad = jnp.sum(gathered * grads_f[:, None, :], axis=2)  7.11 us
  transfers between devices with their start and end apart: 7, of which 4 were waited for; matrix products, arithmetic and copies ran while one was open for 25% of the time, Pallas kernels for 0%

profile of v4, /device:TPU:6, one launch (start us, length us, event | category | flops | bytes accessed | tf_op | source)
XLA Modules:
  0.0 259.8 jit_solution(13392504869858295214)
XLA Ops:
  8.5 3.4 %mul.50.clone = f32[128,2,2048]{2,1,0:T(2,128)} broadcast(bf16[128,2048]{1,0:T(8,128)(2,1)} %param.7), dimensions={0,2} | broadcast | bytes 2621440 | tf_op jit(solution)/shard_map/mul | solution.py:79
  11.9 3.7 %mul.54 = f32[256,2048]{1,0:T(8,128)} reshape(f32[128,2,2048]{2,1,0:T(2,128)} %mul.50.clone) | data formatting | bytes 4194304 | tf_op jit(solution)/shard_map/mul | solution.py:79
  15.9 3.2 %convolution_convert_fusion = bf16[320,2048]{1,0:T(8,128)(2,1)} fusion(f32[256,2048]{1,0:T(8,128)} %mul.54, f32[256]{0:T(256)S(1)} %mul.52, s32[256]{0:T(256)S(1)} %convert_add_fusion), kind=kOutput, calls=%fused_computation.5 | convolution fusion | flops 337330176 | bytes 3409920 | tf_op jit(solution)/shard_map/dot_general | solution.py:45
  19.1 3.3 %reshape.81 = bf16[32,10,2048]{2,1,0:T(8,128)(2,1)} reshape(bf16[320,2048]{1,0:T(8,128)(2,1)} %convolution_convert_fusion) | data formatting | bytes 2621440 | tf_op jit(solution)/shard_map/reshape | solution.py:46
  22.4 3.3 %fusion.32 = (bf16[32,10,1024]{2,1,0:T(8,128)(2,1)}, bf16[32,10,1024]{2,1,0:T(8,128)(2,1)}) fusion(bf16[32,10,2048]{2,1,0:T(8,128)(2,1)} %reshape.81), kind=kLoop, calls=%fused_computation.40 | loop fusion | bytes 2621440 | tf_op jit(solution)/shard_map/slice | solution.py:60
  25.7 17.3 %all-to-all-start.1 = ((bf16[32,10,1024]{2,1,0:T(8,128)(2,1)}), bf16[32,10,1024]{2,1,0:T(8,128)(2,1)}, u32[]{:S(2)}, u32[]{:S(2)}) async-start(bf16[32,10,1024]{2,1,0:T(8,128)(2,1)} %get-tuple-element.16), calls=%async_computation.1 | async-start | bytes 2097152 | tf_op jit(solution)/shard_map/all_to_all | solution.py:61
  43.1 2.2 copy.11
  45.3 9.8 %reshape_reshape.3 = bf16[320,16,2,24]{3,2,1,0:T(2,128)(2,1)} reshape(bf16[1,1,32,10,768]{4,3,2,1,0:T(8,128)(2,1)} %copy.11) | data formatting | bytes 983040 | tf_op jit(solution)/shard_map/reshape;reshape | solution.py:50
  55.2 8.9 %all-to-all-done.1 = bf16[32,10,1024]{2,1,0:T(8,128)(2,1)} async-done(((bf16[32,10,1024]{2,1,0:T(8,128)(2,1)}), bf16[32,10,1024]{2,1,0:T(8,128)(2,1)}, u32[]{:S(2)}, u32[]{:S(2)}) %all-to-all-start.1) | async-done | bytes 655392 | tf_op jit(solution)/shard_map/all_to_all | solution.py:61
  68.2 10.2 %constant_dynamic-slice_fusion.1 = (bf16[320,16,1,24]{3,2,1,0:T(2,128)(2,1)}, bf16[320,16,1,24]{3,2,1,0:T(2,128)(2,1)}) fusion(bf16[320,16,2,24]{3,2,1,0:T(2,128)(2,1)} %reshape_reshape.3, s32[]{:T(128)S(6)} %select_n.7, s32[]{:T(128)S(6)} %select_n.8), kind=kLoop, calls=%fused_computation.36 | loop fusion | bytes 983048 | tf_op jit(solution)/shard_map/jit(dynamic_index_in_dim)/dynamic_slice | solution.py:51
  78.5 5.8 %copy.17 = bf16[320,16,1,24]{0,3,2,1:T(8,128)(2,1)} copy(bf16[320,16,1,24]{3,2,1,0:T(2,128)(2,1)} %get-tuple-element.15) | data formatting | bytes 491520 | tf_op jit(solution)/shard_map/jit(dynamic_index_in_dim)/dynamic_slice | solution.py:52
  84.2 2.4 collective-permute-start
  86.6 4.7 %copy.16 = bf16[320,16,1,24]{0,3,1,2:T(8,128)(2,1)S(1)} copy(bf16[320,16,1,24]{3,2,1,0:T(2,128)(2,1)} %get-tuple-element.14) | data formatting | bytes 491520 | tf_op jit(solution)/shard_map/jit(dynamic_index_in_dim)/dynamic_slice | solution.py:51
  91.4 3.4 %fusion.10 = f32[384,1024]{1,0:T(8,128)} fusion(bf16[320,1024]{1,0:T(8,128)(2,1)} %collective-permute-done.1, bf16[320,1024]{1,0:T(8,128)(2,1)} %reshape.82, bf16[320,384]{0,1:T(8,128)(2,1)} %bitcast.3, bf16[320,384]{0,1:T(8,128)(2,1)S(1)} %bitcast.16), kind=kOutput, calls=%fused_computation.12 | convolution fusion | flops 506920960 | bytes 3375104 | tf_op jit(solution)/shard_map/sh,sd->hd/dot_general | solution.py:66
  94.8 33.9 %all_to_all.15 = bf16[32,10,1024]{2,1,0:T(8,128)(2,1)} all-to-all(bf16[32,10,1024]{2,1,0:T(8,128)(2,1)} %get-tuple-element.17), channel_id=1, replica_groups=mesh['z'=16,'core'=2,'expert'=32] {'expert'}, dimensions={0} | all-to-all | bytes 1310720 | tf_op jit(solution)/shard_map/all_to_all | solution.py:61
  135.1 3.4 %fusion.14 = f32[384,1024]{1,0:T(8,128)} fusion(bf16[320,1024]{1,0:T(8,128)(2,1)} %collective-permute-done.2, bf16[320,1024]{1,0:T(8,128)(2,1)} %reshape.83, bf16[320,384]{0,1:T(8,128)(2,1)} %bitcast.3, bf16[320,384]{0,1:T(8,128)(2,1)S(1)} %bitcast.17), kind=kOutput, calls=%fused_computation.16 | convolution fusion | flops 506920960 | bytes 3375104 | tf_op jit(solution)/shard_map/sh,sd->hd/dot_general | solution.py:66
  138.5 3.3 %fusion.4 = bf16[320,2048]{1,0:T(8,128)(2,1)} fusion(bf16[320,768]{1,0:T(8,128)(2,1)} %reshape.78, bf16[1,768,2048]{2,1,0:T(8,128)(2,1)S(1)} %copy-done), kind=kOutput, calls=%fused_computation.4 | convolution fusion | flops 1007288320 | bytes 4947968 | tf_op jit(solution)/shard_map/dot_general | solution.py:37
  141.8 3.3 %reshape.79 = bf16[32,10,2048]{2,1,0:T(8,128)(2,1)} reshape(bf16[320,2048]{1,0:T(8,128)(2,1)} %fusion.4) | data formatting | bytes 2621440 | tf_op jit(solution)/shard_map/reshape | solution.py:38
  145.2 5.6 %all-to-all-start = ((bf16[32,10,2048]{2,1,0:T(8,128)(2,1)}), bf16[32,10,2048]{2,1,0:T(8,128)(2,1)}, u32[]{:S(2)}, u32[]{:S(2)}) async-start(bf16[32,10,2048]{2,1,0:T(8,128)(2,1)} %reshape.79), calls=%async_computation | async-start | bytes 4194304 | tf_op jit(solution)/shard_map/all_to_all | solution.py:70
  153.2 3.3 %fusion.18 = bf16[320,768]{1,0:T(8,128)(2,1)} fusion(bf16[1,768,2048]{2,1,0:T(8,128)(2,1)S(1)} %copy-done, bf16[320,1024]{1,0:T(8,128)(2,1)} %reshape.83, bf16[320,1024]{1,0:T(8,128)(2,1)} %reshape.82), kind=kOutput, calls=%fused_computation.20 | convolution fusion | flops 1009500160 | bytes 4947968 | tf_op jit(solution)/shard_map/sd,hd->sh/dot_general | solution.py:80
  160.6 39.9 %all-to-all-done = bf16[32,10,2048]{2,1,0:T(8,128)(2,1)} async-done(((bf16[32,10,2048]{2,1,0:T(8,128)(2,1)}), bf16[32,10,2048]{2,1,0:T(8,128)(2,1)}, u32[]{:S(2)}, u32[]{:S(2)}) %all-to-all-start) | async-done | bytes 1310752 | tf_op jit(solution)/shard_map/all_to_all | solution.py:70
  200.5 3.6 %reshape.85 = bf16[320,2048,1]{1,0,2:T(8,128)(2,1)} reshape(bf16[32,10,2048]{2,1,0:T(8,128)(2,1)} %all-to-all-done) | data formatting | bytes 2621440 | tf_op jit(solution)/shard_map/reshape | solution.py:74
  204.1 3.4 %multiply_reduce_fusion = (f32[128,2]{0,1:T(2,128)}, bf16[128,2048]{1,0:T(8,128)(2,1)}) fusion(f32[128,2048]{1,0:T(8,128)} %convert_element_type.31, f32[128,2]{0,1:T(2,128)S(1)} %copy-done.1, bf16[320,2048,1]{1,0,2:T(8,128)(2,1)} %reshape.85, pred[128,2,320]{2,1,0:T(4,128)(4,1)S(1)} %eq.47), kind=kOutput, calls=%fused_computation.7 | convolution fusion | flops 337379072 | bytes 2967552 | tf_op jit(solution)/shard_map/sr,sd->rd/dot_general | solution.py:71
  207.5 43.8 %reduce-scatter.5.cloned.1.call-done = f32[24,1024]{1,0:T(8,128)} async-done(((f32[384,1024]{1,0:T(8,128)}), f32[24,1024]{1,0:T(8,128)}) %reduce-scatter.5.cloned.1.call-update) | async-done | bytes 98320 | tf_op jit(solution)/shard_map/reduce_scatter | solution.py:67
  (29 shorter events, 20.4 us)
Async XLA Ops:
  7.2 131.4 %copy-start = (bf16[1,768,2048]{2,1,0:T(8,128)(2,1)S(1)}, bf16[1,768,2048]{2,1,0:T(8,128)(2,1)}, u32[]{:S(2)}) copy-start(bf16[1,768,2048]{2,1,0:T(8,128)(2,1)} %param.8) | copy-start | bytes 9437188
  11.9 3.7 %copy-start.1 = (f32[128,2]{0,1:T(2,128)S(1)}, f32[128,2]{0,1:T(2,128)}, u32[]{:S(2)}) copy-start(f32[128,2]{0,1:T(2,128)} %param.6) | copy-start | bytes 3076
  25.7 38.4 %all-to-all-start.1 = ((bf16[32,10,1024]{2,1,0:T(8,128)(2,1)}), bf16[32,10,1024]{2,1,0:T(8,128)(2,1)}, u32[]{:S(2)}, u32[]{:S(2)}) async-start(bf16[32,10,1024]{2,1,0:T(8,128)(2,1)} %get-tuple-element.16), calls=%async_computation.1 | async-start | bytes 2097152 | tf_op jit(solution)/shard_map/all_to_all | solution.py:61
  43.0 164.5 %reduce-scatter.3.cloned.1.call-start = ((), (), s32[]{:S(2)}) async-start(), calls=%async_computation.5 | async-start | bytes 1671168 | tf_op jit(solution)/shard_map/reduce_scatter | solution.py:67
  66.1 25.2 %collective-permute-start.1 = (bf16[320,1024]{1,0:T(8,128)(2,1)}, bf16[320,1024]{1,0:T(8,128)(2,1)}, u32[]{:S(2)}, u32[]{:S(2)}) collective-permute-start(bf16[320,1024]{1,0:T(8,128)(2,1)} %reshape.82), channel_id=1, source_target_pairs={{0,32},{32,0},{1,33},{33,1},{2,34},{34,2},{3,35},{35,3},{4,36},{36... | collective-permute-start | bytes 1966088 | tf_op jit(solution)/shard_map/ppermute | solution.py:64
  84.2 7.1 %collective-permute-start = (bf16[320,16,24]{0,2,1:T(8,128)(2,1)}, bf16[320,16,24]{0,2,1:T(8,128)(2,1)}, u32[]{:S(2)}, u32[]{:S(2)}) collective-permute-start(bf16[320,16,24]{0,2,1:T(8,128)(2,1)} %bitcast.2), channel_id=1, source_target_pairs={{0,32},{32,0},{1,33},{33,1},{2,34},{34,2},{3,35},{35,3},{4,36},{36... | collective-permute-start | bytes 737288 | tf_op jit(solution)/shard_map/ppermute | solution.py:53
  94.8 156.5 %reduce-scatter.5.cloned.1.call-start = ((), (), s32[]{:S(2)}) async-start(), calls=%async_computation.6 | async-start | bytes 1671168 | tf_op jit(solution)/shard_map/reduce_scatter | solution.py:67
  130.8 4.3 %collective-permute-start.2 = (bf16[320,1024]{1,0:T(8,128)(2,1)}, bf16[320,1024]{1,0:T(8,128)(2,1)}, u32[]{:S(2)}, u32[]{:S(2)}) collective-permute-start(bf16[320,1024]{1,0:T(8,128)(2,1)} %reshape.83), channel_id=1, source_target_pairs={{0,32},{32,0},{1,33},{33,1},{2,34},{34,2},{3,35},{35,3},{4,36},{36... | collective-permute-start | bytes 1966088 | tf_op jit(solution)/shard_map/ppermute | solution.py:64
  145.2 55.4 %all-to-all-start = ((bf16[32,10,2048]{2,1,0:T(8,128)(2,1)}), bf16[32,10,2048]{2,1,0:T(8,128)(2,1)}, u32[]{:S(2)}, u32[]{:S(2)}) async-start(bf16[32,10,2048]{2,1,0:T(8,128)(2,1)} %reshape.79), calls=%async_computation | async-start | bytes 4194304 | tf_op jit(solution)/shard_map/all_to_all | solution.py:70
Sparse Core Ops, SparseCore 0:
  94.9 79.7 reduce-scatter.2
  178.0 73.1 reduce-scatter.4

commit v5 on v3

--- a/solution.py
+++ b/solution.py
@@ -30,12 +30,15 @@
     give = lax.dynamic_index_in_dim(parts, 1 - c, axis=0, keepdims=False)
     got = lax.ppermute(give, "core", [(0, 1), (1, 0)])
     chip_sum = (keep + got).reshape(rows // cores, -1)
-    return lax.psum_scatter(chip_sum, "z", scatter_dimension=0, tiled=True)
+    near = lax.psum_scatter(chip_sum, "z_lo", scatter_dimension=0, tiled=True)
+    return lax.psum_scatter(near, "z_hi", scatter_dimension=0, tiled=True)
 
 
 def on_device(route_ids, gate_values, out_grad, down_weight, hidden):
     experts = lax.axis_size("expert")
-    chips = lax.axis_size("z")
+    z_hi = lax.axis_size("z_hi")
+    z_lo = lax.axis_size("z_lo")
+    chips = z_hi * z_lo
     cores = lax.axis_size("core")
     capacity = hidden.shape[3]
     inner_width = hidden.shape[4]
@@ -59,7 +62,9 @@
     grad_rows = incoming.reshape(-1, feature_width)
     block = inner_width // (chips * cores)
     rows_perm = (
-        rows_in.reshape(-1, chips, cores, block).transpose(0, 2, 1, 3).reshape(-1, inner_width)
+        rows_in.reshape(-1, z_hi, z_lo, cores, block)
+        .transpose(0, 3, 2, 1, 4)
+        .reshape(-1, inner_width)
     )
     partial_term = jnp.einsum(
         "sh,sd->hd", rows_perm, grad_rows, preferred_element_type=jnp.float32
@@ -83,20 +88,24 @@
 def solution(mesh):
     n_dp = mesh.shape["dp"]
     n_ex = mesh.shape["expert"]
-    sub = Mesh(mesh.devices.reshape(n_dp // 2, 2, n_ex), ("z", "core", "expert"))
-    tok = ("z", "core", "expert")
+    n_lo = 4 if n_dp % 8 == 0 else 1
+    sub = Mesh(
+        mesh.devices.reshape(n_dp // (2 * n_lo), n_lo, 2, n_ex), ("z_hi", "z_lo", "core", "expert")
+    )
+    dp = ("z_hi", "z_lo", "core")
+    tok = dp + ("expert",)
     in_specs = (
         P(tok, None),
         P(tok, None),
         P(tok, None),
         P("expert", None, None),
-        P(("z", "core"), "expert", None, None, None),
+        P(dp, "expert", None, None, None),
     )
     out_specs = (
         P(tok, None),
         P(tok, None),
-        P(("z", "core"), "expert", None, None, None),
-        P("expert", ("z", "core"), None),
+        P(dp, "expert", None, None, None),
+        P("expert", dp, None),
     )
     return jax.shard_map(
         on_device, mesh=sub, in_specs=in_specs, out_specs=out_specs, check_vma=False

time: 200 us -> 253 us (1.26)
  waiting for transfers between devices: 83.9 us -> 137 us
    reduce_scatter x1 -> x2, waiting for transfers between devices: 13.5 us -> 106 us  [the longest x1 62.8 us: reduce_over_dp(): near = lax.psum_scatter(chip_sum, 'z_lo', scatter_dimension=0, tiled=True)]
    all_to_all x1, waiting for transfers between devices: 39.8 us -> 0.01 us  [on_device(): lax.all_to_all(expert_out, 'expert', split_axis=0, concat_axis=0, tiled=T...]
  transfers between devices with their start and end apart: 4 -> 5, of which waited for: 4 -> 4; matrix products, arithmetic and copies ran while one was open for 22% -> 17% of each run, Pallas kernels for 0% -> 0%
where the time goes in v5:
time: 253 us; the launch traced here: 252 us
  waiting for transfers between devices  137 us (54%)
  local copies, waits for them, and re-layouts  51 us (20%)
  starting transfers between devices  25.9 us (10%)
  matrix products  16.8 us (7%)
  between operations  14.1 us (6%)
  other arithmetic  7.47 us (3%)
    reduce_scatter x1, waiting for transfers between devices, reduce_over_dp(): near = lax.psum_scatter(chip_sum, 'z_lo', scatter_dimension=0, tiled=True)  62.8 us
    reduce_scatter x1, waiting for transfers between devices, reduce_over_dp(): return lax.psum_scatter(near, 'z_hi', scatter_dimension=0, tiled=True)  43.5 us
    all_to_all x1, waiting for transfers between devices, on_device(): lax.all_to_all(outgoing, 'expert', split_axis=0, concat_axis=0, tiled=True)  24.6 us
    all_to_all x1, starting transfers between devices, on_device(): lax.all_to_all(outgoing, 'expert', split_axis=0, concat_axis=0, tiled=True)  17.5 us
    another operation x1, local copies, waits for them, and re-layouts, on_device(): rows_in.reshape(-1, z_hi, z_lo, cores, block).transpose(0, 3, 2, 1, 4)  9.86 us
    unnamed x10, local copies, waits for them, and re-layouts  7.62 us
    mul x2, local copies, waits for them, and re-layouts, on_device(): gate_grad = jnp.sum(gathered * grads_f[:, None, :], axis=2)  7.11 us
    all_to_all x1, starting transfers between devices, on_device(): lax.all_to_all(expert_out, 'expert', split_axis=0, concat_axis=0, tiled=T...  6.29 us
  transfers between devices with their start and end apart: 5, of which 4 were waited for; matrix products, arithmetic and copies ran while one was open for 17% of the time, Pallas kernels for 0%

profile of v5, /device:TPU:6, one launch (start us, length us, event | category | flops | bytes accessed | tf_op | source)
XLA Modules:
  0.0 252.1 jit_solution(2038567897161937791)
XLA Ops:
  9.4 3.4 %mul.50.clone = f32[128,2,2048]{2,1,0:T(2,128)} broadcast(bf16[128,2048]{1,0:T(8,128)(2,1)} %param.7), dimensions={0,2} | broadcast | bytes 2621440 | tf_op jit(solution)/shard_map/mul | solution.py:82
  12.8 3.7 %mul.54 = f32[256,2048]{1,0:T(8,128)} reshape(f32[128,2,2048]{2,1,0:T(2,128)} %mul.50.clone) | data formatting | bytes 4194304 | tf_op jit(solution)/shard_map/mul | solution.py:82
  16.5 3.3 %convolution_convert_fusion = bf16[320,2048]{1,0:T(8,128)(2,1)} fusion(f32[256,2048]{1,0:T(8,128)} %mul.54, f32[256]{0:T(256)S(1)} %mul.52, s32[256]{0:T(256)S(1)} %convert_add_fusion), kind=kOutput, calls=%fused_computation.7 | convolution fusion | flops 337330176 | bytes 3409920 | tf_op jit(solution)/shard_map/dot_general | solution.py:59
  19.8 3.3 %reshape.83 = bf16[32,10,2048]{2,1,0:T(8,128)(2,1)} reshape(bf16[320,2048]{1,0:T(8,128)(2,1)} %convolution_convert_fusion) | data formatting | bytes 2621440 | tf_op jit(solution)/shard_map/reshape | solution.py:60
  23.1 17.5 %all-to-all-start.1 = ((bf16[32,10,2048]{2,1,0:T(8,128)(2,1)}), bf16[32,10,2048]{2,1,0:T(8,128)(2,1)}, u32[]{:S(2)}, u32[]{:S(2)}) async-start(bf16[32,10,2048]{2,1,0:T(8,128)(2,1)} %reshape.83), calls=%async_computation.1 | async-start | bytes 4194304 | tf_op jit(solution)/shard_map/all_to_all | solution.py:61
  40.6 2.2 copy.11
  42.8 9.9 %reshape_reshape.3 = bf16[320,4,4,2,24]{4,3,2,1,0:T(2,128)(2,1)} reshape(bf16[1,1,32,10,768]{4,3,2,1,0:T(8,128)(2,1)} %copy.11) | data formatting | bytes 983040 | tf_op jit(solution)/shard_map/reshape;reshape | solution.py:65
  52.7 6.0 %copy.16 = bf16[320,2,4,4,24]{0,4,3,2,1:T(8,128)(2,1)} copy(bf16[320,2,4,4,24]{4,1,2,3,0:T(2,128)(2,1)} %bitcast.28) | data formatting | bytes 983040 | tf_op jit(solution)/shard_map/transpose | solution.py:66
  58.7 24.6 %all-to-all-done.1 = bf16[32,10,2048]{2,1,0:T(8,128)(2,1)} async-done(((bf16[32,10,2048]{2,1,0:T(8,128)(2,1)}), bf16[32,10,2048]{2,1,0:T(8,128)(2,1)}, u32[]{:S(2)}, u32[]{:S(2)}) %all-to-all-start.1) | async-done | bytes 1310752 | tf_op jit(solution)/shard_map/all_to_all | solution.py:61
  83.3 3.6 %reshape.84 = bf16[320,2048]{1,0:T(8,128)(2,1)} reshape(bf16[32,10,2048]{2,1,0:T(8,128)(2,1)} %all-to-all-done.1) | data formatting | bytes 2621440 | tf_op jit(solution)/shard_map/reshape | solution.py:62
  86.8 3.3 %fusion.16 = f32[2048,768]{0,1:T(8,128)S(1)} fusion(bf16[320,768]{0,1:T(8,128)(2,1)} %bitcast.29, bf16[320,2048]{1,0:T(8,128)(2,1)} %reshape.84), kind=kOutput, calls=%fused_computation.24 | convolution fusion | flops 1006632960 | bytes 8093696 | tf_op jit(solution)/shard_map/sh,sd->hd/dot_general | solution.py:69
  95.7 6.0 %collective-permute-done = f32[16,24,2048]{2,1,0:T(8,128)} collective-permute-done((f32[16,24,2048]{2,1,0:T(8,128)}, f32[16,24,2048]{2,1,0:T(8,128)}, u32[]{:S(2)}, u32[]{:S(2)}) %collective-permute-start) | collective-permute-done | bytes 3145760 | tf_op jit(solution)/shard_map/ppermute | solution.py:31
  101.7 5.2 %bitcast_add_fusion = f32[16,24,2048]{2,1,0:T(8,128)} fusion(f32[16,24,2048]{2,1,0:T(8,128)} %collective-permute-done, f32[2,16,24,2048]{3,2,1,0:T(8,128)} %bitcast.26, s32[]{:T(128)S(6)} %select_n.7), kind=kLoop, calls=%fused_computation | loop fusion | flops 786432 | bytes 9437188 | tf_op jit(solution)/shard_map/add | solution.py:32
  109.0 3.3 %fusion.4 = bf16[320,2048]{1,0:T(8,128)(2,1)} fusion(bf16[320,768]{1,0:T(8,128)(2,1)} %reshape.80, bf16[1,768,2048]{2,1,0:T(8,128)(2,1)S(1)} %copy-done), kind=kOutput, calls=%fused_computation.6 | convolution fusion | flops 1007288320 | bytes 4947968 | tf_op jit(solution)/shard_map/dot_general | solution.py:51
  112.3 3.3 %reshape.81 = bf16[32,10,2048]{2,1,0:T(8,128)(2,1)} reshape(bf16[320,2048]{1,0:T(8,128)(2,1)} %fusion.4) | data formatting | bytes 2621440 | tf_op jit(solution)/shard_map/reshape | solution.py:52
  115.6 6.3 %all-to-all-start = ((bf16[32,10,2048]{2,1,0:T(8,128)(2,1)}), bf16[32,10,2048]{2,1,0:T(8,128)(2,1)}, u32[]{:S(2)}, u32[]{:S(2)}) async-start(bf16[32,10,2048]{2,1,0:T(8,128)(2,1)} %reshape.81), calls=%async_computation | async-start | bytes 4194304 | tf_op jit(solution)/shard_map/all_to_all | solution.py:73
  122.1 62.8 %reduce-scatter.3.cloned.1.call-done = f32[96,2048]{1,0:T(8,128)} async-done(((f32[384,2048]{1,0:T(8,128)}), f32[96,2048]{1,0:T(8,128)}) %reduce-scatter.3.cloned.1.call-update) | async-done | bytes 786448 | tf_op jit(solution)/shard_map/reduce_scatter | solution.py:33
  184.9 2.1 convert_element_type.31
  187.3 3.3 %fusion.7 = bf16[320,768]{1,0:T(8,128)(2,1)} fusion(bf16[320,2048]{1,0:T(8,128)(2,1)} %reshape.84, bf16[1,768,2048]{2,1,0:T(8,128)(2,1)S(1)} %copy-done), kind=kOutput, calls=%fused_computation.11 | convolution fusion | flops 1006878720 | bytes 4947968 | tf_op jit(solution)/shard_map/sd,hd->sh/dot_general | solution.py:83
  190.6 2.0 reshape.85
  192.7 2.1 copy.17
  194.8 3.6 %reshape.89 = bf16[320,2048,1]{1,0,2:T(8,128)(2,1)} reshape(bf16[32,10,2048]{2,1,0:T(8,128)(2,1)} %all-to-all-done) | data formatting | bytes 2621440 | tf_op jit(solution)/shard_map/reshape | solution.py:77
  198.4 3.4 %multiply_reduce_fusion = (f32[128,2]{0,1:T(2,128)}, bf16[128,2048]{1,0:T(8,128)(2,1)}) fusion(f32[128,2048]{1,0:T(8,128)} %convert_element_type.31, f32[128,2]{0,1:T(2,128)S(1)} %copy-done.2, bf16[320,2048,1]{1,0,2:T(8,128)(2,1)} %reshape.89, pred[128,2,320]{2,1,0:T(4,128)(4,1)S(1)} %eq.47), kind=kOutput, calls=%fused_computation.9 | convolution fusion | flops 337379072 | bytes 2967552 | tf_op jit(solution)/shard_map/sr,sd->rd/dot_general | solution.py:74
  201.8 43.5 %reduce-scatter.5.cloned.1.call-done = f32[24,2048]{1,0:T(8,128)} async-done(((f32[96,2048]{1,0:T(8,128)}), f32[24,2048]{1,0:T(8,128)}) %reduce-scatter.5.cloned.1.call-update) | async-done | bytes 196624 | tf_op jit(solution)/shard_map/reduce_scatter | solution.py:34
  (22 shorter events, 10.4 us)
Async XLA Ops:
  7.2 101.8 %copy-start = (bf16[1,768,2048]{2,1,0:T(8,128)(2,1)S(1)}, bf16[1,768,2048]{2,1,0:T(8,128)(2,1)}, u32[]{:S(2)}) copy-start(bf16[1,768,2048]{2,1,0:T(8,128)(2,1)} %param.8) | copy-start | bytes 9437188
  23.1 60.2 %all-to-all-start.1 = ((bf16[32,10,2048]{2,1,0:T(8,128)(2,1)}), bf16[32,10,2048]{2,1,0:T(8,128)(2,1)}, u32[]{:S(2)}, u32[]{:S(2)}) async-start(bf16[32,10,2048]{2,1,0:T(8,128)(2,1)} %reshape.83), calls=%async_computation.1 | async-start | bytes 4194304 | tf_op jit(solution)/shard_map/all_to_all | solution.py:61
  40.6 144.3 %reduce-scatter.3.cloned.1.call-start = ((), (), s32[]{:S(2)}) async-start(), calls=%async_computation.4 | async-start | bytes 3932160 | tf_op jit(solution)/shard_map/reduce_scatter | solution.py:33
  90.1 3.7 %copy-start.1 = (f32[2048,768]{0,1:T(8,128)}, f32[2048,768]{0,1:T(8,128)S(1)}, u32[]{:S(2)}) copy-start(f32[2048,768]{0,1:T(8,128)S(1)} %fusion.16) | copy-start | bytes 18874372
  93.8 7.9 %collective-permute-start = (f32[16,24,2048]{2,1,0:T(8,128)}, f32[16,24,2048]{2,1,0:T(8,128)}, u32[]{:S(2)}, u32[]{:S(2)}) collective-permute-start(f32[16,24,2048]{2,1,0:T(8,128)} %dynamic-slice_bitcast_fusion), channel_id=1, source_target_pairs={{0,32},{32,0},{1,33},{33,1},{2,34},{34,2},{3,35},{35,3},{4,36},{36... | collective-permute-start | bytes 9437192 | tf_op jit(solution)/shard_map/ppermute | solution.py:31
  115.6 79.2 %all-to-all-start = ((bf16[32,10,2048]{2,1,0:T(8,128)(2,1)}), bf16[32,10,2048]{2,1,0:T(8,128)(2,1)}, u32[]{:S(2)}, u32[]{:S(2)}) async-start(bf16[32,10,2048]{2,1,0:T(8,128)(2,1)} %reshape.81), calls=%async_computation | async-start | bytes 4194304 | tf_op jit(solution)/shard_map/all_to_all | solution.py:73
  121.9 123.4 %reduce-scatter.5.cloned.1.call-start = ((), (), s32[]{:S(2)}) async-start(), calls=%async_computation.5 | async-start | bytes 983040 | tf_op jit(solution)/shard_map/reduce_scatter | solution.py:34
  192.7 5.7 %copy-start.2 = (f32[128,2]{0,1:T(2,128)S(1)}, f32[128,2]{0,1:T(2,128)}, u32[]{:S(2)}) copy-start(f32[128,2]{0,1:T(2,128)} %param.6) | copy-start | bytes 3076
Sparse Core Ops, SparseCore 0:
  107.1 77.8 reduce-scatter.2
  188.9 56.3 reduce-scatter.4

commit v6 on v1

--- a/solution.py
+++ b/solution.py
@@ -37,24 +37,31 @@
     expert_out = jnp.dot(rows_in, weight_mat, preferred_element_type=jnp.float32)
     expert_out = expert_out.astype(jnp.bfloat16).reshape(experts, capacity, feature_width)
     grads_f = out_grad.astype(jnp.float32)
-    scaled = (
-        (gate_values[:, :, None] * grads_f[:, None, :])
-        .reshape(-1, feature_width)
-        .astype(jnp.bfloat16)
-    )
-    outgoing = jnp.dot(slot_map, scaled, preferred_element_type=jnp.float32)
-    outgoing = outgoing.astype(jnp.bfloat16).reshape(experts, capacity, feature_width)
+    by_token = slot_map.reshape(-1, tok_rows, routes)
+    token_hot = jnp.sum(by_token, axis=2)
+    slot_gate = jnp.sum(by_token.astype(jnp.float32) * gate_values[None], axis=(1, 2))
+    slot_grads = jnp.dot(token_hot, out_grad, preferred_element_type=jnp.float32)
+    outgoing = (slot_gate[:, None] * slot_grads).astype(jnp.bfloat16)
+    outgoing = outgoing.reshape(experts, capacity, feature_width)
     incoming = lax.all_to_all(outgoing, "expert", split_axis=0, concat_axis=0, tiled=True)
     grad_rows = incoming.reshape(-1, feature_width)
     block = inner_width // (chips * cores)
-    rows_perm = (
-        rows_in.reshape(-1, chips, cores, block).transpose(0, 2, 1, 3).reshape(-1, inner_width)
-    )
-    partial_term = jnp.einsum(
-        "sh,sd->hd", rows_perm, grad_rows, preferred_element_type=jnp.float32
-    )
-    half = lax.psum_scatter(partial_term, "core", scatter_dimension=0, tiled=True)
-    weight_grad = lax.psum_scatter(half, "z", scatter_dimension=0, tiled=True)
+    c = lax.axis_index("core")
+    swap = [(0, 1), (1, 0)]
+    col_of = jnp.arange(inner_width, dtype=jnp.int32).reshape(chips, cores, block)
+
+    def columns(core):
+        pick = col_of[:, 0, :].reshape(-1) + core * block
+        sel = (jnp.arange(inner_width, dtype=jnp.int32)[:, None] == pick[None, :])
+        return jnp.dot(rows_in, sel.astype(jnp.bfloat16), preferred_element_type=jnp.float32)
+
+    mine_cols = columns(c).astype(jnp.bfloat16)
+    got_cols = lax.ppermute(columns(1 - c).astype(jnp.bfloat16), "core", swap)
+    both_cols = jnp.concatenate([mine_cols, got_cols], axis=0)
+    partner = lax.ppermute(grad_rows, "core", swap)
+    both = jnp.concatenate([grad_rows, partner], axis=0)
+    chip_part = jnp.einsum("sh,sd->hd", both_cols, both, preferred_element_type=jnp.float32)
+    weight_grad = lax.psum_scatter(chip_part, "z", scatter_dimension=0, tiled=True)
     returned = lax.all_to_all(expert_out, "expert", split_axis=0, concat_axis=0, tiled=True)
     gathered = jnp.einsum(
         "sr,sd->rd",

time: 223 us -> 190 us (0.85)
  blocking collectives: 0 us -> 60.8 us
  waiting for transfers between devices: 103 us -> 55.2 us
  local copies, waits for them, and re-layouts: 55.4 us -> 23.8 us
  starting transfers between devices: 27.4 us -> 9.96 us
    all_to_all x0 -> x1, blocking collectives: none -> 60.8 us  [on_device(): lax.all_to_all(outgoing, 'expert', split_axis=0, concat_axis=0, tiled=True)]
    all_to_all x1 -> x0, waiting for transfers between devices: 24.6 us -> none  [on_device(): lax.all_to_all(outgoing, 'expert', split_axis=0, concat_axis=0, tiled=True)]
    all_to_all x1 -> x0, starting transfers between devices: 17.4 us -> none  [on_device(): lax.all_to_all(outgoing, 'expert', split_axis=0, concat_axis=0, tiled=True)]
    reduce_scatter x1, waiting for transfers between devices: 31.2 us -> 15.3 us  [on_device(): lax.psum_scatter(chip_part, 'z', scatter_dimension=0, tiled=True)]
    another operation x1 -> x0, local copies, waits for them, and re-layouts: 9.85 us -> none  [on_device(): rows_in.reshape(-1, chips, cores, block).transpose(0, 2, 1, 3)]
    unnamed x11 -> x7, local copies, waits for them, and re-layouts: 14 us -> 5.23 us
    unnamed x3 -> x1, waiting for transfers between devices: 7.57 us -> 0.02 us
    mul x3 -> x0, local copies, waits for them, and re-layouts: 7.24 us -> none  [the longest x2 7.1 us: on_device(): gate_grad = jnp.sum(gathered * grads_f[:, None, :], axis=2)]
  transfers between devices with their start and end apart: 4 -> 4, of which waited for: 4 -> 2; matrix products, arithmetic and copies ran while one was open for 20% -> 17% of each run, Pallas kernels for 0% -> 0%
where the time goes in v6:
time: 190 us; the launch traced here: 189 us
  blocking collectives  60.8 us (32%)
  waiting for transfers between devices  55.2 us (29%)
  local copies, waits for them, and re-layouts  23.8 us (13%)
  matrix products  21.3 us (11%)
  between operations  14.2 us (7%)
  starting transfers between devices  9.96 us (5%)
  other arithmetic  3.97 us (2%)
    all_to_all x1, blocking collectives, on_device(): lax.all_to_all(outgoing, 'expert', split_axis=0, concat_axis=0, tiled=True)  60.8 us
    all_to_all x1, waiting for transfers between devices, on_device(): lax.all_to_all(expert_out, 'expert', split_axis=0, concat_axis=0, tiled=T...  39.9 us
    reduce_scatter x1, waiting for transfers between devices, on_device(): lax.psum_scatter(chip_part, 'z', scatter_dimension=0, tiled=True)  15.3 us
    all_to_all x1, starting transfers between devices, on_device(): lax.all_to_all(expert_out, 'expert', split_axis=0, concat_axis=0, tiled=T...  5.62 us
    unnamed x7, local copies, waits for them, and re-layouts  5.23 us
    dot_general x1, matrix products, on_device(): jnp.einsum('sh,sd->hd', both_cols, both, preferred_element_type=jnp.float32)  4.8 us
  transfers between devices with their start and end apart: 4, of which 2 were waited for; matrix products, arithmetic and copies ran while one was open for 17% of the time, Pallas kernels for 0%

profile of v6, /device:TPU:6, one launch (start us, length us, event | category | flops | bytes accessed | tf_op | source)
XLA Modules:
  0.0 189.2 jit_solution(10643358850476923123)
XLA Ops:
  7.2 0.9 copy.26
  9.5 0.8 multiply_reduce_fusion.2
  10.3 2.6 %fusion.4 = bf16[320,2048]{1,0:T(8,128)(2,1)} fusion(bf16[320,128]{1,0:T(8,128)(2,1)S(1)} %fusion.26, bf16[128,2048]{1,0:T(8,128)(2,1)} %param.7, f32[320]{0:T(512)S(1)} %multiply_reduce_fusion.2), kind=kOutput, calls=%fused_computation.5 | convolution fusion | flops 169082880 | bytes 1918208 | tf_op jit(solution)/shard_map/dot_general | solution.py:43
  12.9 3.3 %reshape.119 = bf16[32,10,2048]{2,1,0:T(8,128)(2,1)} reshape(bf16[320,2048]{1,0:T(8,128)(2,1)} %fusion.4) | data formatting | bytes 2621440 | tf_op jit(solution)/shard_map/reshape | solution.py:45
  16.3 60.8 %all_to_all.10 = bf16[32,10,2048]{2,1,0:T(8,128)(2,1)} all-to-all(bf16[32,10,2048]{2,1,0:T(8,128)(2,1)} %reshape.119), channel_id=1, replica_groups=mesh['z'=16,'core'=2,'expert'=32] {'expert'}, dimensions={0} | all-to-all | bytes 2621440 | tf_op jit(solution)/shard_map/all_to_all | solution.py:46
  77.1 3.6 %reshape.120 = bf16[320,2048]{1,0:T(8,128)(2,1)} reshape(bf16[32,10,2048]{2,1,0:T(8,128)(2,1)} %all_to_all.10) | data formatting | bytes 2621440 | tf_op jit(solution)/shard_map/reshape | solution.py:47
  80.7 1.9 %collective-permute-start.1 = (bf16[320,2048]{1,0:T(8,128)(2,1)}, bf16[320,2048]{1,0:T(8,128)(2,1)}, u32[]{:S(2)}, u32[]{:S(2)}) collective-permute-start(bf16[320,2048]{1,0:T(8,128)(2,1)} %reshape.120), channel_id=1, source_target_pairs={{0,32},{32,0},{1,33},{33,1},{2,34},{34,2},{3,35},{35,3},{4,36},{36... | collective-permute-start | bytes 3932168 | tf_op jit(solution)/shard_map/ppermute | solution.py:61
  82.8 2.2 %copy.27 = bf16[1,1,32,10,768]{4,3,2,1,0:T(8,128)(2,1)} copy(bf16[1,1,32,10,768]{4,2,3,1,0:T(8,128)(2,1)} %param.9) | data formatting | bytes 983040 | tf_op args[4]
  85.0 2.0 %reshape.116 = bf16[320,768]{1,0:T(8,128)(2,1)} reshape(bf16[1,1,32,10,768]{4,3,2,1,0:T(8,128)(2,1)} %copy.27) | data formatting | bytes 983040 | tf_op jit(solution)/shard_map/reshape | solution.py:36
  87.0 2.2 %fusion.16 = bf16[320,384]{1,0:T(8,128)(2,1)} fusion(bf16[320,768]{1,0:T(8,128)(2,1)} %reshape.116, s32[384]{0:T(512)S(1)} %add.47), kind=kOutput, calls=%fused_computation.19 | convolution fusion | flops 189161472 | bytes 738816 | tf_op jit(solution)/shard_map/dot_general | solution.py:56
  89.2 2.4 %collective-permute-start = (bf16[320,384]{1,0:T(8,128)(2,1)}, bf16[320,384]{1,0:T(8,128)(2,1)S(1)}, u32[]{:S(2)}, u32[]{:S(2)}) collective-permute-start(bf16[320,384]{1,0:T(8,128)(2,1)} %fusion.16), channel_id=1, source_target_pairs={{0,32},{32,0},{1,33},{33,1},{2,34},{34,2},{3,35},{35,3},{4,36},{36... | collective-permute-start | bytes 737288 | tf_op jit(solution)/shard_map/ppermute | solution.py:59
  91.7 1.5 fusion.15
  93.2 4.8 %fusion.8 = f32[384,2048]{1,0:T(8,128)} fusion(bf16[320,2048]{1,0:T(8,128)(2,1)} %collective-permute-done.1, bf16[320,2048]{1,0:T(8,128)(2,1)} %reshape.120, bf16[320,384]{1,0:T(8,128)(2,1)S(1)} %collective-permute-done, bf16[320,384]{1,0:T(8,128)(2,1)S(1)} %fusion.15), kind=kOutput, calls=%fused_computation.7 | convolution fusion | flops 1012858880 | bytes 6258688 | tf_op jit(solution)/shard_map/sh,sd->hd/dot_general | solution.py:63
  98.0 3.3 %fusion.5 = bf16[320,2048]{1,0:T(8,128)(2,1)} fusion(bf16[320,768]{1,0:T(8,128)(2,1)} %reshape.116, bf16[1,768,2048]{2,1,0:T(8,128)(2,1)S(1)} %copy-done), kind=kOutput, calls=%fused_computation.6 | convolution fusion | flops 1007288320 | bytes 4947968 | tf_op jit(solution)/shard_map/dot_general | solution.py:37
  101.3 3.4 %reshape.117 = bf16[32,10,2048]{2,1,0:T(8,128)(2,1)} reshape(bf16[320,2048]{1,0:T(8,128)(2,1)} %fusion.5) | data formatting | bytes 2621440 | tf_op jit(solution)/shard_map/reshape | solution.py:38
  104.7 5.6 %all-to-all-start = ((bf16[32,10,2048]{2,1,0:T(8,128)(2,1)}), bf16[32,10,2048]{2,1,0:T(8,128)(2,1)}, u32[]{:S(2)}, u32[]{:S(2)}) async-start(bf16[32,10,2048]{2,1,0:T(8,128)(2,1)} %reshape.117), calls=%async_computation | async-start | bytes 4194304 | tf_op jit(solution)/shard_map/all_to_all | solution.py:65
  110.3 2.2 %convert_element_type.54 = f32[128,2048]{1,0:T(8,128)} convert(bf16[128,2048]{1,0:T(8,128)(2,1)} %param.7) | non-fusion elementwise | flops 262144 | bytes 1572864 | tf_op jit(solution)/shard_map/convert_element_type | solution.py:39
  112.8 3.3 %fusion.12 = bf16[320,768]{1,0:T(8,128)(2,1)} fusion(bf16[320,2048]{1,0:T(8,128)(2,1)} %reshape.120, bf16[1,768,2048]{2,1,0:T(8,128)(2,1)S(1)} %copy-done), kind=kOutput, calls=%fused_computation.13 | convolution fusion | flops 1006878720 | bytes 4947968 | tf_op jit(solution)/shard_map/sd,hd->sh/dot_general | solution.py:75
  116.1 2.0 %reshape.121 = bf16[1,1,32,10,768]{4,3,2,1,0:T(8,128)(2,1)} reshape(bf16[320,768]{1,0:T(8,128)(2,1)} %fusion.12) | data formatting | bytes 983040 | tf_op jit(solution)/shard_map/reshape | solution.py:76
  118.1 2.1 %copy.30 = bf16[1,1,32,10,768]{4,2,3,1,0:T(8,128)(2,1)} copy(bf16[1,1,32,10,768]{4,3,2,1,0:T(8,128)(2,1)} %reshape.121) | data formatting | bytes 983040
  120.2 39.9 %all-to-all-done = bf16[32,10,2048]{2,1,0:T(8,128)(2,1)} async-done(((bf16[32,10,2048]{2,1,0:T(8,128)(2,1)}), bf16[32,10,2048]{2,1,0:T(8,128)(2,1)}, u32[]{:S(2)}, u32[]{:S(2)}) %all-to-all-start) | async-done | bytes 1310752 | tf_op jit(solution)/shard_map/all_to_all | solution.py:65
  160.1 3.6 %reshape.128 = bf16[320,2048,1]{1,0,2:T(8,128)(2,1)} reshape(bf16[32,10,2048]{2,1,0:T(8,128)(2,1)} %all-to-all-done) | data formatting | bytes 2621440 | tf_op jit(solution)/shard_map/reshape | solution.py:69
  163.6 3.4 %multiply_reduce_fusion = (f32[128,2]{0,1:T(2,128)}, bf16[128,2048]{1,0:T(8,128)(2,1)}) fusion(f32[128,2048]{1,0:T(8,128)} %convert_element_type.54, f32[128,2]{0,1:T(2,128)S(1)} %copy-done.1, bf16[320,2048,1]{1,0,2:T(8,128)(2,1)} %reshape.128, pred[128,2,320]{2,1,0:T(4,128)(4,1)S(1)} %eq.74), kind=kOutput, calls=%fused_computation.11 | convolution fusion | flops 337379072 | bytes 2967552 | tf_op jit(solution)/shard_map/sr,sd->rd/dot_general | solution.py:66
  167.1 15.3 %reduce-scatter.2.cloned.1.call-done = f32[24,2048]{1,0:T(8,128)} async-done(((f32[384,2048]{1,0:T(8,128)}), f32[24,2048]{1,0:T(8,128)}) %reduce-scatter.2.cloned.1.call-update) | async-done | bytes 196624 | tf_op jit(solution)/shard_map/reduce_scatter | solution.py:64
  (21 shorter events, 1.8 us)
Async XLA Ops:
  7.2 90.9 %copy-start = (bf16[1,768,2048]{2,1,0:T(8,128)(2,1)S(1)}, bf16[1,768,2048]{2,1,0:T(8,128)(2,1)}, u32[]{:S(2)}) copy-start(bf16[1,768,2048]{2,1,0:T(8,128)(2,1)} %param.8) | copy-start | bytes 9437188
  7.2 175.2 %reduce-scatter.2.cloned.1.call-start = ((), (), s32[]{:S(2)}) async-start(), calls=%async_computation.3 | async-start | bytes 3342336 | tf_op jit(solution)/shard_map/reduce_scatter | solution.py:64
  80.7 12.5 %collective-permute-start.1 = (bf16[320,2048]{1,0:T(8,128)(2,1)}, bf16[320,2048]{1,0:T(8,128)(2,1)}, u32[]{:S(2)}, u32[]{:S(2)}) collective-permute-start(bf16[320,2048]{1,0:T(8,128)(2,1)} %reshape.120), channel_id=1, source_target_pairs={{0,32},{32,0},{1,33},{33,1},{2,34},{34,2},{3,35},{35,3},{4,36},{36... | collective-permute-start | bytes 3932168 | tf_op jit(solution)/shard_map/ppermute | solution.py:61
  89.2 4.0 %collective-permute-start = (bf16[320,384]{1,0:T(8,128)(2,1)}, bf16[320,384]{1,0:T(8,128)(2,1)S(1)}, u32[]{:S(2)}, u32[]{:S(2)}) collective-permute-start(bf16[320,384]{1,0:T(8,128)(2,1)} %fusion.16), channel_id=1, source_target_pairs={{0,32},{32,0},{1,33},{33,1},{2,34},{34,2},{3,35},{35,3},{4,36},{36... | collective-permute-start | bytes 737288 | tf_op jit(solution)/shard_map/ppermute | solution.py:59
  104.7 55.4 %all-to-all-start = ((bf16[32,10,2048]{2,1,0:T(8,128)(2,1)}), bf16[32,10,2048]{2,1,0:T(8,128)(2,1)}, u32[]{:S(2)}, u32[]{:S(2)}) async-start(bf16[32,10,2048]{2,1,0:T(8,128)(2,1)} %reshape.117), calls=%async_computation | async-start | bytes 4194304 | tf_op jit(solution)/shard_map/all_to_all | solution.py:65
  118.1 45.5 %copy-start.1 = (f32[128,2]{0,1:T(2,128)S(1)}, f32[128,2]{0,1:T(2,128)}, u32[]{:S(2)}) copy-start(f32[128,2]{0,1:T(2,128)} %param.6) | copy-start | bytes 3076
Sparse Core Ops, SparseCore 0:
  98.1 84.1 reduce-scatter.1

commit v7 on v6

--- a/solution.py
+++ b/solution.py
@@ -33,18 +33,16 @@
     routes = route_ids.shape[1]
     slot_map = slot_table(route_ids, experts, capacity)
     weight_mat = down_weight[0]
-    rows_in = hidden.reshape(-1, inner_width)
-    expert_out = jnp.dot(rows_in, weight_mat, preferred_element_type=jnp.float32)
-    expert_out = expert_out.astype(jnp.bfloat16).reshape(experts, capacity, feature_width)
+    rows_in = hidden[0, 0]
+    expert_out = jnp.einsum("sch,hd->scd", rows_in, weight_mat, preferred_element_type=jnp.float32)
+    expert_out = expert_out.astype(jnp.bfloat16)
     grads_f = out_grad.astype(jnp.float32)
-    by_token = slot_map.reshape(-1, tok_rows, routes)
-    token_hot = jnp.sum(by_token, axis=2)
-    slot_gate = jnp.sum(by_token.astype(jnp.float32) * gate_values[None], axis=(1, 2))
-    slot_grads = jnp.dot(token_hot, out_grad, preferred_element_type=jnp.float32)
-    outgoing = (slot_gate[:, None] * slot_grads).astype(jnp.bfloat16)
-    outgoing = outgoing.reshape(experts, capacity, feature_width)
-    incoming = lax.all_to_all(outgoing, "expert", split_axis=0, concat_axis=0, tiled=True)
-    grad_rows = incoming.reshape(-1, feature_width)
+    by_token = slot_map.reshape(experts, capacity, tok_rows, routes)
+    token_hot = jnp.sum(by_token, axis=3)
+    slot_gate = jnp.sum(by_token.astype(jnp.float32) * gate_values[None, None], axis=(2, 3))
+    slot_grads = jnp.einsum("ect,td->ecd", token_hot, out_grad, preferred_element_type=jnp.float32)
+    outgoing = (slot_gate[:, :, None] * slot_grads).astype(jnp.bfloat16)
+    grad_rows = lax.all_to_all(outgoing, "expert", split_axis=0, concat_axis=0, tiled=True)
     block = inner_width // (chips * cores)
     c = lax.axis_index("core")
     swap = [(0, 1), (1, 0)]
@@ -53,26 +51,30 @@
     def columns(core):
         pick = col_of[:, 0, :].reshape(-1) + core * block
         sel = (jnp.arange(inner_width, dtype=jnp.int32)[:, None] == pick[None, :])
-        return jnp.dot(rows_in, sel.astype(jnp.bfloat16), preferred_element_type=jnp.float32)
+        return jnp.einsum(
+            "sch,hj->scj", rows_in, sel.astype(jnp.bfloat16), preferred_element_type=jnp.float32
+        )
 
     mine_cols = columns(c).astype(jnp.bfloat16)
     got_cols = lax.ppermute(columns(1 - c).astype(jnp.bfloat16), "core", swap)
     both_cols = jnp.concatenate([mine_cols, got_cols], axis=0)
     partner = lax.ppermute(grad_rows, "core", swap)
     both = jnp.concatenate([grad_rows, partner], axis=0)
-    chip_part = jnp.einsum("sh,sd->hd", both_cols, both, preferred_element_type=jnp.float32)
+    chip_part = jnp.einsum("sch,scd->hd", both_cols, both, preferred_element_type=jnp.float32)
     weight_grad = lax.psum_scatter(chip_part, "z", scatter_dimension=0, tiled=True)
     returned = lax.all_to_all(expert_out, "expert", split_axis=0, concat_axis=0, tiled=True)
     gathered = jnp.einsum(
-        "sr,sd->rd",
-        slot_map,
-        returned.reshape(-1, feature_width),
+        "ecr,ecd->rd",
+        slot_map.reshape(experts, capacity, -1),
+        returned,
         preferred_element_type=jnp.float32,
     )
     gathered = gathered.reshape(tok_rows, routes, feature_width)
     mixed_out = jnp.sum(gate_values[:, :, None] * gathered, axis=1).astype(jnp.bfloat16)
     gate_grad = jnp.sum(gathered * grads_f[:, None, :], axis=2)
-    hidden_grad = jnp.einsum("sd,hd->sh", grad_rows, weight_mat, preferred_element_type=jnp.float32)
+    hidden_grad = jnp.einsum(
+        "scd,hd->sch", grad_rows, weight_mat, preferred_element_type=jnp.float32
+    )
     hidden_grad = hidden_grad.astype(jnp.bfloat16).reshape(hidden.shape)
     return (mixed_out, gate_grad, hidden_grad, weight_grad[None])
 

time: 190 us -> 180 us (0.947)
  local copies, waits for them, and re-layouts: 23.8 us -> 6.24 us
  waiting for transfers between devices: 55.2 us -> 64.7 us
    reshape x6 -> x0, local copies, waits for them, and re-layouts: 17.9 us -> none  [the longest x1 3.61 us: on_device(): grad_rows = incoming.reshape(-1, feature_width)]
    all_to_all x1, waiting for transfers between devices: 39.9 us -> 47.5 us  [on_device(): lax.all_to_all(expert_out, 'expert', split_axis=0, concat_axis=0, tiled=T...]
    unnamed x7 -> x5, local copies, waits for them, and re-layouts: 5.23 us -> 0.95 us
    convert_element_type x0 -> x2, local copies, waits for them, and re-layouts: none -> 2.96 us  [the longest x1 2.16 us: on_device(): expert_out = expert_out.astype(jnp.bfloat16)]
  transfers between devices with their start and end apart: 4 -> 4, of which waited for: 2 -> 2; matrix products, arithmetic and copies ran while one was open for 17% -> 10% of each run, Pallas kernels for 0% -> 0%
where the time goes in v7:
time: 180 us; the launch traced here: 179 us
  waiting for transfers between devices  64.7 us (36%)
  blocking collectives  60.2 us (33%)
  matrix products  19.8 us (11%)
  between operations  14.2 us (8%)
  starting transfers between devices  10.4 us (6%)
  local copies, waits for them, and re-layouts  6.24 us (3%)
  other arithmetic  3.97 us (2%)
    all_to_all x1, blocking collectives, on_device(): lax.all_to_all(outgoing, 'expert', split_axis=0, concat_axis=0, tiled=True)  60.2 us
    all_to_all x1, waiting for transfers between devices, on_device(): lax.all_to_all(expert_out, 'expert', split_axis=0, concat_axis=0, tiled=T...  47.5 us
    reduce_scatter x1, waiting for transfers between devices, on_device(): lax.psum_scatter(chip_part, 'z', scatter_dimension=0, tiled=True)  17.1 us
    all_to_all x1, starting transfers between devices, on_device(): lax.all_to_all(expert_out, 'expert', split_axis=0, concat_axis=0, tiled=T...  6.09 us
    dot_general x1, matrix products, on_device(): jnp.einsum('sch,scd->hd', both_cols, both, preferred_element_type=jnp.flo...  4.8 us
    dot_general x1, matrix products, on_device(): jnp.einsum('ecr,ecd->rd', slot_map.reshape(experts, capacity, -1), return...  4.07 us
    dot_general x2, matrix products, columns(): jnp.einsum('sch,hj->scj', rows_in, sel.astype(jnp.bfloat16), preferred_el...  3.67 us
  transfers between devices with their start and end apart: 4, of which 2 were waited for; matrix products, arithmetic and copies ran while one was open for 10% of the time, Pallas kernels for 0%

profile of v7, /device:TPU:6, one launch (start us, length us, event | category | flops | bytes accessed | tf_op | source)
XLA Modules:
  0.0 179.5 jit_solution(18060435211460521241)
XLA Ops:
  7.2 0.9 copy.38
  8.2 0.1 reshape.94
  8.3 0.2 fusion.29
  8.5 0.1 convert_element_type.53
  8.7 0.7 multiply_add_fusion.2
  9.4 0.1 fusion.40
  9.6 0.9 multiply_reduce_fusion.2
  10.4 1.5 fusion.4
  12.0 0.8 copy.42
  12.8 60.2 %all_to_all.10 = bf16[32,10,2048]{2,1,0:T(8,128)(2,1)S(1)} all-to-all(bf16[32,10,2048]{2,1,0:T(8,128)(2,1)S(1)} %copy.42), channel_id=1, replica_groups=mesh['z'=16,'core'=2,'expert'=32] {'expert'}, dimensions={0} | all-to-all | bytes 2621440 | tf_op jit(solution)/shard_map/all_to_all | solution.py:45
  73.0 1.8 %copy.43 = bf16[32,10,2048]{2,0,1:T(8,128)(2,1)} copy(bf16[32,10,2048]{2,1,0:T(8,128)(2,1)S(1)} %all_to_all.10) | data formatting | bytes 2621440 | tf_op jit(solution)/shard_map/all_to_all | solution.py:45
  74.8 1.9 %collective-permute-start.1 = (bf16[32,10,2048]{2,0,1:T(8,128)(2,1)}, bf16[32,10,2048]{2,0,1:T(8,128)(2,1)}, u32[]{:S(2)}, u32[]{:S(2)}) collective-permute-start(bf16[32,10,2048]{2,0,1:T(8,128)(2,1)} %copy.43), channel_id=1, source_target_pairs={{0,32},{32,0},{1,33},{33,1},{2,34},{34,2},{3,35},{35,3},{4,36},{36... | collective-permute-start | bytes 3932168 | tf_op jit(solution)/shard_map/ppermute | solution.py:61
  76.9 2.2 %fusion.26 = bf16[32,10,384]{2,0,1:T(8,128)(2,1)} fusion(s32[384]{0:T(512)S(1)} %add.51, bf16[1,1,32,10,768]{4,2,3,1,0:T(8,128)(2,1)} %param.9), kind=kOutput, calls=%fused_computation.25 | convolution fusion | flops 189161472 | bytes 738816 | tf_op jit(solution)/shard_map/sch,hj->scj/dot_general | solution.py:54
  79.1 2.4 %collective-permute-start = (bf16[32,10,384]{2,0,1:T(8,128)(2,1)}, bf16[32,10,384]{2,0,1:T(8,128)(2,1)S(1)}, u32[]{:S(2)}, u32[]{:S(2)}) collective-permute-start(bf16[32,10,384]{2,0,1:T(8,128)(2,1)} %fusion.26), channel_id=1, source_target_pairs={{0,32},{32,0},{1,33},{33,1},{2,34},{34,2},{3,35},{35,3},{4,36},{36... | collective-permute-start | bytes 737288 | tf_op jit(solution)/shard_map/ppermute | solution.py:59
  81.6 1.5 fusion.23
  83.1 4.8 %convolution_bitcast_fusion = f32[384,2048]{1,0:T(8,128)} fusion(bf16[32,10,2048]{2,0,1:T(8,128)(2,1)} %collective-permute-done.1, bf16[32,10,2048]{2,0,1:T(8,128)(2,1)} %copy.43, bf16[32,10,384]{2,0,1:T(8,128)(2,1)S(1)} %collective-permute-done, bf16[32,10,384]{2,0,1:T(8,128)(2,1)S(1)} %fusion.23), kind=kOutput, calls=%fused_computation.4 | convolution fusion | flops 1012858880 | bytes 6258688 | tf_op jit(solution)/shard_map/sch,scd->hd/dot_general | solution.py:63
  87.9 2.2 %fusion.5 = bf16[32,10,2048]{2,0,1:T(8,128)(2,1)S(1)} fusion(bf16[1,768,2048]{2,1,0:T(8,128)(2,1)S(1)} %copy-done, bf16[1,1,32,10,768]{4,2,3,1,0:T(8,128)(2,1)} %param.9), kind=kOutput, calls=%fused_computation.8 | convolution fusion | flops 1007288320 | bytes 4947968 | tf_op jit(solution)/shard_map/sch,hd->scd/dot_general | solution.py:37
  90.1 2.2 %copy.40 = bf16[32,10,2048]{2,1,0:T(8,128)(2,1)} copy(bf16[32,10,2048]{2,0,1:T(8,128)(2,1)S(1)} %fusion.5) | data formatting | bytes 2621440 | tf_op jit(solution)/shard_map/convert_element_type | solution.py:38
  92.3 6.1 %all-to-all-start = ((bf16[32,10,2048]{2,1,0:T(8,128)(2,1)}), bf16[32,10,2048]{2,1,0:T(8,128)(2,1)}, u32[]{:S(2)}, u32[]{:S(2)}) async-start(bf16[32,10,2048]{2,1,0:T(8,128)(2,1)} %copy.40), calls=%async_computation | async-start | bytes 4194304 | tf_op jit(solution)/shard_map/all_to_all | solution.py:65
  98.4 2.2 %convert_element_type.56 = f32[128,2048]{1,0:T(8,128)} convert(bf16[128,2048]{1,0:T(8,128)(2,1)} %param.7) | non-fusion elementwise | flops 262144 | bytes 1572864 | tf_op jit(solution)/shard_map/convert_element_type | solution.py:39
  100.6 47.5 %all-to-all-done = bf16[32,10,2048]{2,1,0:T(8,128)(2,1)} async-done(((bf16[32,10,2048]{2,1,0:T(8,128)(2,1)}), bf16[32,10,2048]{2,1,0:T(8,128)(2,1)}, u32[]{:S(2)}, u32[]{:S(2)}) %all-to-all-start) | async-done | bytes 1310752 | tf_op jit(solution)/shard_map/all_to_all | solution.py:65
  148.1 4.1 %multiply_reduce_fusion = (f32[128,2]{0,1:T(2,128)}, bf16[128,2048]{1,0:T(8,128)(2,1)}) fusion(f32[128,2048]{1,0:T(8,128)} %convert_element_type.56, f32[128,2]{0,1:T(2,128)S(1)} %copy-done.1, bf16[32,10,2048]{2,1,0:T(8,128)(2,1)} %all-to-all-done, s32[128,2]{0,1:T(2,128)S(1)} %multiply_add_fusion.2, s32[10,32]{1,0:T(8,128)S(1)} %multiply_add_fusion.1), kind=kOutput, calls=%fused_computation.12 | convolution fusion | flops 337460992 | bytes 2887936 | tf_op jit(solution)/shard_map/ecr,ecd->rd/dot_general | solution.py:66
  152.2 3.3 %fusion.16 = bf16[1,1,32,10,768]{4,2,3,1,0:T(8,128)(2,1)} fusion(bf16[32,10,2048]{2,0,1:T(8,128)(2,1)} %copy.43, bf16[1,768,2048]{2,1,0:T(8,128)(2,1)S(1)} %copy-done), kind=kOutput, calls=%fused_computation.17 | convolution fusion | flops 1006878720 | bytes 4947968 | tf_op jit(solution)/shard_map/scd,hd->sch/dot_general | solution.py:75
  155.5 17.1 %reduce-scatter.2.cloned.1.call-done = f32[24,2048]{1,0:T(8,128)} async-done(((f32[384,2048]{1,0:T(8,128)}), f32[24,2048]{1,0:T(8,128)}) %reduce-scatter.2.cloned.1.call-update) | async-done | bytes 196624 | tf_op jit(solution)/shard_map/reduce_scatter | solution.py:64
  (15 shorter events, 0.4 us)
Async XLA Ops:
  7.2 80.7 %copy-start = (bf16[1,768,2048]{2,1,0:T(8,128)(2,1)S(1)}, bf16[1,768,2048]{2,1,0:T(8,128)(2,1)}, u32[]{:S(2)}) copy-start(bf16[1,768,2048]{2,1,0:T(8,128)(2,1)} %param.8) | copy-start | bytes 9437188
  7.2 165.5 %reduce-scatter.2.cloned.1.call-start = ((), (), s32[]{:S(2)}) async-start(), calls=%async_computation.3 | async-start | bytes 3342336 | tf_op jit(solution)/shard_map/reduce_scatter | solution.py:64
  74.8 8.3 %collective-permute-start.1 = (bf16[32,10,2048]{2,0,1:T(8,128)(2,1)}, bf16[32,10,2048]{2,0,1:T(8,128)(2,1)}, u32[]{:S(2)}, u32[]{:S(2)}) collective-permute-start(bf16[32,10,2048]{2,0,1:T(8,128)(2,1)} %copy.43), channel_id=1, source_target_pairs={{0,32},{32,0},{1,33},{33,1},{2,34},{34,2},{3,35},{35,3},{4,36},{36... | collective-permute-start | bytes 3932168 | tf_op jit(solution)/shard_map/ppermute | solution.py:61
  79.1 4.0 %collective-permute-start = (bf16[32,10,384]{2,0,1:T(8,128)(2,1)}, bf16[32,10,384]{2,0,1:T(8,128)(2,1)S(1)}, u32[]{:S(2)}, u32[]{:S(2)}) collective-permute-start(bf16[32,10,384]{2,0,1:T(8,128)(2,1)} %fusion.26), channel_id=1, source_target_pairs={{0,32},{32,0},{1,33},{33,1},{2,34},{34,2},{3,35},{35,3},{4,36},{36... | collective-permute-start | bytes 737288 | tf_op jit(solution)/shard_map/ppermute | solution.py:59
  92.3 55.9 %copy-start.1 = (f32[128,2]{0,1:T(2,128)S(1)}, f32[128,2]{0,1:T(2,128)}, u32[]{:S(2)}) copy-start(f32[128,2]{0,1:T(2,128)} %param.6) | copy-start | bytes 3076
  92.3 55.8 %all-to-all-start = ((bf16[32,10,2048]{2,1,0:T(8,128)(2,1)}), bf16[32,10,2048]{2,1,0:T(8,128)(2,1)}, u32[]{:S(2)}, u32[]{:S(2)}) async-start(bf16[32,10,2048]{2,1,0:T(8,128)(2,1)} %copy.40), calls=%async_computation | async-start | bytes 4194304 | tf_op jit(solution)/shard_map/all_to_all | solution.py:65
Sparse Core Ops, SparseCore 0:
  88.0 84.5 reduce-scatter.1

commit v8 on v7

--- a/solution.py
+++ b/solution.py
@@ -61,7 +61,8 @@
     partner = lax.ppermute(grad_rows, "core", swap)
     both = jnp.concatenate([grad_rows, partner], axis=0)
     chip_part = jnp.einsum("sch,scd->hd", both_cols, both, preferred_element_type=jnp.float32)
-    weight_grad = lax.psum_scatter(chip_part, "z", scatter_dimension=0, tiled=True)
+    chip_total = lax.psum(chip_part, "z")
+    weight_grad = lax.dynamic_slice_in_dim(chip_total, lax.axis_index("z") * block, block, axis=0)
     returned = lax.all_to_all(expert_out, "expert", split_axis=0, concat_axis=0, tiled=True)
     gathered = jnp.einsum(
         "ecr,ecd->rd",

time: 180 us -> 271 us (1.51)
  waiting for transfers between devices: 64.7 us -> 155 us
    psum x0 -> x1, waiting for transfers between devices: none -> 114 us  [on_device(): chip_total = lax.psum(chip_part, 'z')]
    reduce_scatter x1 -> x0, waiting for transfers between devices: 17.1 us -> none  [on_device(): lax.psum_scatter(chip_part, 'z', scatter_dimension=0, tiled=True)]
    all_to_all x1, waiting for transfers between devices: 47.5 us -> 41.2 us  [on_device(): lax.all_to_all(expert_out, 'expert', split_axis=0, concat_axis=0, tiled=T...]
  transfers between devices with their start and end apart: 4 -> 4, of which waited for: 2 -> 2; matrix products, arithmetic and copies ran while one was open for 10% -> 8% of each run, Pallas kernels for 0% -> 0%
where the time goes in v8:
time: 271 us; the launch traced here: 270 us
  waiting for transfers between devices  155 us (57%)
  blocking collectives  60.2 us (22%)
  matrix products  18.9 us (7%)
  between operations  14.2 us (5%)
  starting transfers between devices  10.3 us (4%)
  local copies, waits for them, and re-layouts  7.86 us (3%)
  other arithmetic  3.9 us (1%)
    psum x1, waiting for transfers between devices, on_device(): chip_total = lax.psum(chip_part, 'z')  114 us
    all_to_all x1, blocking collectives, on_device(): lax.all_to_all(outgoing, 'expert', split_axis=0, concat_axis=0, tiled=True)  60.2 us
    all_to_all x1, waiting for transfers between devices, on_device(): lax.all_to_all(expert_out, 'expert', split_axis=0, concat_axis=0, tiled=T...  41.2 us
    all_to_all x1, starting transfers between devices, on_device(): lax.all_to_all(expert_out, 'expert', split_axis=0, concat_axis=0, tiled=T...  5.96 us
  transfers between devices with their start and end apart: 4, of which 2 were waited for; matrix products, arithmetic and copies ran while one was open for 8% of the time, Pallas kernels for 0%

profile of v8, /device:TPU:6, one launch (start us, length us, event | category | flops | bytes accessed | tf_op | source)
XLA Modules:
  0.0 270.4 jit_solution(13922846771134079916)
XLA Ops:
  7.2 0.9 copy.38
  8.1 0.1 reshape.94
  8.3 0.2 fusion.29
  8.5 0.1 convert_element_type.53
  8.7 0.7 multiply_add_fusion.2
  9.5 0.9 multiply_reduce_fusion.2
  10.4 1.5 fusion.4
  11.9 0.8 copy.42
  12.8 60.2 %all_to_all.10 = bf16[32,10,2048]{2,1,0:T(8,128)(2,1)S(1)} all-to-all(bf16[32,10,2048]{2,1,0:T(8,128)(2,1)S(1)} %copy.42), channel_id=1, replica_groups=mesh['z'=16,'core'=2,'expert'=32] {'expert'}, dimensions={0} | all-to-all | bytes 2621440 | tf_op jit(solution)/shard_map/all_to_all | solution.py:45
  72.9 1.8 copy.43
  74.7 1.9 collective-permute-start.1
  76.8 2.2 fusion.26
  79.1 2.4 collective-permute-start
  81.5 1.2 fusion.5
  82.7 2.2 copy.40
  84.9 6.0 %all-to-all-start = ((bf16[32,10,2048]{2,1,0:T(8,128)(2,1)}), bf16[32,10,2048]{2,1,0:T(8,128)(2,1)}, u32[]{:S(2)}, u32[]{:S(2)}) async-start(bf16[32,10,2048]{2,1,0:T(8,128)(2,1)} %copy.40), calls=%async_computation | async-start | bytes 4194304 | tf_op jit(solution)/shard_map/all_to_all | solution.py:66
  91.0 1.5 fusion.23
  92.5 4.8 %convolution_bitcast_fusion = f32[384,2048]{1,0:T(8,128)} fusion(bf16[32,10,2048]{2,0,1:T(8,128)(2,1)} %collective-permute-done.1, bf16[32,10,2048]{2,0,1:T(8,128)(2,1)} %copy.43, bf16[32,10,384]{2,0,1:T(8,128)(2,1)S(1)} %collective-permute-done, bf16[32,10,384]{2,0,1:T(8,128)(2,1)S(1)} %fusion.23), kind=kOutput, calls=%fused_computation.4 | convolution fusion | flops 1012858880 | bytes 6258688 | tf_op jit(solution)/shard_map/sch,scd->hd/dot_general | solution.py:63
  97.3 2.1 convert_element_type.56
  99.5 41.2 %all-to-all-done = bf16[32,10,2048]{2,1,0:T(8,128)(2,1)} async-done(((bf16[32,10,2048]{2,1,0:T(8,128)(2,1)}), bf16[32,10,2048]{2,1,0:T(8,128)(2,1)}, u32[]{:S(2)}, u32[]{:S(2)}) %all-to-all-start) | async-done | bytes 1310752 | tf_op jit(solution)/shard_map/all_to_all | solution.py:66
  140.7 4.1 %multiply_reduce_fusion = (f32[128,2]{0,1:T(2,128)}, bf16[128,2048]{1,0:T(8,128)(2,1)}) fusion(f32[128,2048]{1,0:T(8,128)} %convert_element_type.56, f32[128,2]{0,1:T(2,128)S(1)} %copy-done.1, bf16[32,10,2048]{2,1,0:T(8,128)(2,1)} %all-to-all-done, s32[128,2]{0,1:T(2,128)S(1)} %multiply_add_fusion.2, s32[10,32]{1,0:T(8,128)S(1)} %multiply_add_fusion.1), kind=kOutput, calls=%fused_computation.12 | convolution fusion | flops 337460992 | bytes 2887936 | tf_op jit(solution)/shard_map/ecr,ecd->rd/dot_general | solution.py:67
  144.7 3.3 %fusion.16 = bf16[1,1,32,10,768]{4,2,3,1,0:T(8,128)(2,1)} fusion(bf16[32,10,2048]{2,0,1:T(8,128)(2,1)} %copy.43, bf16[1,768,2048]{2,1,0:T(8,128)(2,1)S(1)} %copy-done), kind=kOutput, calls=%fused_computation.17 | convolution fusion | flops 1006878720 | bytes 4947968 | tf_op jit(solution)/shard_map/scd,hd->sch/dot_general | solution.py:76
  148.0 113.9 %all-reduce.2.cloned.1.call-done = f32[384,2048]{1,0:T(8,128)} async-done(((f32[384,2048]{1,0:T(8,128)}), f32[384,2048]{1,0:T(8,128)}) %all-reduce.2.cloned.1.call-update) | async-done | bytes 3145744 | tf_op jit(solution)/shard_map/psum | solution.py:64
  262.0 1.6 dynamic-slice_bitcast_fusion
  (18 shorter events, 0.5 us)
Async XLA Ops:
  7.2 74.3 %copy-start = (bf16[1,768,2048]{2,1,0:T(8,128)(2,1)S(1)}, bf16[1,768,2048]{2,1,0:T(8,128)(2,1)}, u32[]{:S(2)}) copy-start(bf16[1,768,2048]{2,1,0:T(8,128)(2,1)} %param.8) | copy-start | bytes 9437188
  74.7 17.8 %collective-permute-start.1 = (bf16[32,10,2048]{2,0,1:T(8,128)(2,1)}, bf16[32,10,2048]{2,0,1:T(8,128)(2,1)}, u32[]{:S(2)}, u32[]{:S(2)}) collective-permute-start(bf16[32,10,2048]{2,0,1:T(8,128)(2,1)} %copy.43), channel_id=1, source_target_pairs={{0,32},{32,0},{1,33},{33,1},{2,34},{34,2},{3,35},{35,3},{4,36},{36... | collective-permute-start | bytes 3932168 | tf_op jit(solution)/shard_map/ppermute | solution.py:61
  76.8 4.7 %copy-start.2 = (bf16[1,1,32,10,768]{4,2,3,1,0:T(8,128)(2,1)S(1)}, bf16[1,1,32,10,768]{4,2,3,1,0:T(8,128)(2,1)}, u32[]{:S(2)}) copy-start(bf16[1,1,32,10,768]{4,2,3,1,0:T(8,128)(2,1)} %param.9) | copy-start | bytes 1474564
  79.1 13.4 %collective-permute-start = (bf16[32,10,384]{2,0,1:T(8,128)(2,1)}, bf16[32,10,384]{2,0,1:T(8,128)(2,1)S(1)}, u32[]{:S(2)}, u32[]{:S(2)}) collective-permute-start(bf16[32,10,384]{2,0,1:T(8,128)(2,1)} %fusion.26), channel_id=1, source_target_pairs={{0,32},{32,0},{1,33},{33,1},{2,34},{34,2},{3,35},{35,3},{4,36},{36... | collective-permute-start | bytes 737288 | tf_op jit(solution)/shard_map/ppermute | solution.py:59
  84.9 55.8 %all-to-all-start = ((bf16[32,10,2048]{2,1,0:T(8,128)(2,1)}), bf16[32,10,2048]{2,1,0:T(8,128)(2,1)}, u32[]{:S(2)}, u32[]{:S(2)}) async-start(bf16[32,10,2048]{2,1,0:T(8,128)(2,1)} %copy.40), calls=%async_computation | async-start | bytes 4194304 | tf_op jit(solution)/shard_map/all_to_all | solution.py:66
  90.8 171.1 %all-reduce.2.cloned.1.call-start = ((), (), s32[]{:S(2)}) async-start(), calls=%async_computation.2 | async-start | bytes 6291456 | tf_op jit(solution)/shard_map/psum | solution.py:64
  97.3 43.3 %copy-start.1 = (f32[128,2]{0,1:T(2,128)S(1)}, f32[128,2]{0,1:T(2,128)}, u32[]{:S(2)}) copy-start(f32[128,2]{0,1:T(2,128)} %param.6) | copy-start | bytes 3076
Sparse Core Ops, SparseCore 0:
  97.5 164.4 all-reduce.1

commit v9 on v7

--- a/solution.py
+++ b/solution.py
@@ -57,10 +57,11 @@
 
     mine_cols = columns(c).astype(jnp.bfloat16)
     got_cols = lax.ppermute(columns(1 - c).astype(jnp.bfloat16), "core", swap)
-    both_cols = jnp.concatenate([mine_cols, got_cols], axis=0)
     partner = lax.ppermute(grad_rows, "core", swap)
-    both = jnp.concatenate([grad_rows, partner], axis=0)
-    chip_part = jnp.einsum("sch,scd->hd", both_cols, both, preferred_element_type=jnp.float32)
+    own_part = jnp.einsum("sch,scd->hd", mine_cols, grad_rows, preferred_element_type=jnp.float32)
+    chip_part = own_part + jnp.einsum(
+        "sch,scd->hd", got_cols, partner, preferred_element_type=jnp.float32
+    )
     weight_grad = lax.psum_scatter(chip_part, "z", scatter_dimension=0, tiled=True)
     returned = lax.all_to_all(expert_out, "expert", split_axis=0, concat_axis=0, tiled=True)
     gathered = jnp.einsum(

time: 180 us -> 183 us (1.017)
  matrix products: 19.8 us -> 23.1 us
    dot_general x1 -> x2, matrix products: 4.8 us -> 9.54 us  [the longest x1 4.97 us: on_device(): jnp.einsum('sch,scd->hd', got_cols, partner, preferred_element_type=jnp.f...]
    dot_general x2 -> x1, matrix products: 3.67 us -> 2.19 us  [columns(): jnp.einsum('sch,hj->scj', rows_in, sel.astype(jnp.bfloat16), preferred_el...]
  transfers between devices with their start and end apart: 4 -> 4, of which waited for: 2 -> 2; matrix products, arithmetic and copies ran while one was open for 10% -> 11% of each run, Pallas kernels for 0% -> 0%
where the time goes in v9:
time: 183 us
  waiting for transfers between devices  64.5 us (35%)
  blocking collectives  60.2 us (33%)
  matrix products  23.1 us (13%)
  between operations  14.2 us (8%)
  starting transfers between devices  10.4 us (6%)
  local copies, waits for them, and re-layouts  6.24 us (3%)
  other arithmetic  3.97 us (2%)
    all_to_all x1, blocking collectives, on_device(): lax.all_to_all(outgoing, 'expert', split_axis=0, concat_axis=0, tiled=True)  60.2 us
    all_to_all x1, waiting for transfers between devices, on_device(): lax.all_to_all(expert_out, 'expert', split_axis=0, concat_axis=0, tiled=T...  47.6 us
    reduce_scatter x1, waiting for transfers between devices, on_device(): lax.psum_scatter(chip_part, 'z', scatter_dimension=0, tiled=True)  16.9 us
    all_to_all x1, starting transfers between devices, on_device(): lax.all_to_all(expert_out, 'expert', split_axis=0, concat_axis=0, tiled=T...  6.1 us
    dot_general x1, matrix products, on_device(): jnp.einsum('sch,scd->hd', got_cols, partner, preferred_element_type=jnp.f...  4.97 us
    dot_general x1, matrix products, on_device(): jnp.einsum('sch,scd->hd', mine_cols, grad_rows, preferred_element_type=jn...  4.57 us
    dot_general x1, matrix products, on_device(): jnp.einsum('ecr,ecd->rd', slot_map.reshape(experts, capacity, -1), return...  4.07 us
  transfers between devices with their start and end apart: 4, of which 2 were waited for; matrix products, arithmetic and copies ran while one was open for 11% of the time, Pallas kernels for 0%

profile of v9, /device:TPU:6, one launch (start us, length us, event | category | flops | bytes accessed | tf_op | source)
XLA Modules:
  0.0 182.6 jit_solution(15214587073340296501)
XLA Ops:
  7.2 0.9 copy.38
  8.2 0.1 reshape.94
  8.3 0.2 fusion.26
  8.5 0.1 convert_element_type.53
  8.7 0.7 multiply_add_fusion.2
  9.4 0.1 fusion.39
  9.6 0.9 multiply_reduce_fusion.2
  10.4 1.5 fusion.4
  12.0 0.8 copy.42
  12.8 60.2 %all_to_all.10 = bf16[32,10,2048]{2,1,0:T(8,128)(2,1)S(1)} all-to-all(bf16[32,10,2048]{2,1,0:T(8,128)(2,1)S(1)} %copy.42), channel_id=1, replica_groups=mesh['z'=16,'core'=2,'expert'=32] {'expert'}, dimensions={0} | all-to-all | bytes 2621440 | tf_op jit(solution)/shard_map/all_to_all | solution.py:45
  73.0 1.8 copy.43
  74.8 1.9 %collective-permute-start.1 = (bf16[32,10,2048]{2,0,1:T(8,128)(2,1)}, bf16[32,10,2048]{2,0,1:T(8,128)(2,1)}, u32[]{:S(2)}, u32[]{:S(2)}) collective-permute-start(bf16[32,10,2048]{2,0,1:T(8,128)(2,1)} %copy.43), channel_id=1, source_target_pairs={{0,32},{32,0},{1,33},{33,1},{2,34},{34,2},{3,35},{35,3},{4,36},{36... | collective-permute-start | bytes 3932168 | tf_op jit(solution)/shard_map/ppermute | solution.py:60
  76.9 2.2 %fusion.23 = bf16[32,10,384]{2,0,1:T(8,128)(2,1)} fusion(s32[384]{0:T(512)S(1)} %add.54, bf16[1,1,32,10,768]{4,2,3,1,0:T(8,128)(2,1)} %param.9), kind=kOutput, calls=%fused_computation.22 | convolution fusion | flops 189161472 | bytes 738816 | tf_op jit(solution)/shard_map/sch,hj->scj/dot_general | solution.py:54
  79.0 2.4 %collective-permute-start = (bf16[32,10,384]{2,0,1:T(8,128)(2,1)}, bf16[32,10,384]{2,0,1:T(8,128)(2,1)S(1)}, u32[]{:S(2)}, u32[]{:S(2)}) collective-permute-start(bf16[32,10,384]{2,0,1:T(8,128)(2,1)} %fusion.23), channel_id=1, source_target_pairs={{0,32},{32,0},{1,33},{33,1},{2,34},{34,2},{3,35},{35,3},{4,36},{36... | collective-permute-start | bytes 737288 | tf_op jit(solution)/shard_map/ppermute | solution.py:59
  81.6 4.6 %fusion.28 = f32[384,2048,1]{1,0,2:T(8,128)} fusion(bf16[32,10,2048]{2,0,1:T(8,128)(2,1)} %copy.43, s32[384]{0:T(512)S(1)} %add.51, bf16[1,1,32,10,768]{4,2,3,1,0:T(8,128)(2,1)} %param.9), kind=kOutput, calls=%fused_computation.25 | convolution fusion | flops 692477952 | bytes 4949504 | tf_op jit(solution)/shard_map/sch,scd->hd/dot_general | solution.py:61
  86.2 5.0 %bitcast_add_fusion = f32[384,2048]{1,0:T(8,128)} fusion(f32[384,2048,1]{1,0,2:T(8,128)} %fusion.28, bf16[32,10,384]{2,0,1:T(8,128)(2,1)S(1)} %collective-permute-done, bf16[32,10,2048]{2,0,1:T(8,128)(2,1)} %collective-permute-done.1), kind=kOutput, calls=%fused_computation | convolution fusion | flops 504102912 | bytes 7847936 | tf_op jit(solution)/shard_map/sch,scd->hd/dot_general | solution.py:62
  91.2 2.2 %fusion.5 = bf16[32,10,2048]{2,0,1:T(8,128)(2,1)S(1)} fusion(bf16[1,768,2048]{2,1,0:T(8,128)(2,1)S(1)} %copy-done, bf16[1,1,32,10,768]{4,2,3,1,0:T(8,128)(2,1)} %param.9), kind=kOutput, calls=%fused_computation.8 | convolution fusion | flops 1007288320 | bytes 4947968 | tf_op jit(solution)/shard_map/sch,hd->scd/dot_general | solution.py:37
  93.4 2.2 %copy.40 = bf16[32,10,2048]{2,1,0:T(8,128)(2,1)} copy(bf16[32,10,2048]{2,0,1:T(8,128)(2,1)S(1)} %fusion.5) | data formatting | bytes 2621440 | tf_op jit(solution)/shard_map/convert_element_type | solution.py:38
  95.5 6.1 %all-to-all-start = ((bf16[32,10,2048]{2,1,0:T(8,128)(2,1)}), bf16[32,10,2048]{2,1,0:T(8,128)(2,1)}, u32[]{:S(2)}, u32[]{:S(2)}) async-start(bf16[32,10,2048]{2,1,0:T(8,128)(2,1)} %copy.40), calls=%async_computation | async-start | bytes 4194304 | tf_op jit(solution)/shard_map/all_to_all | solution.py:66
  101.7 2.2 %convert_element_type.56 = f32[128,2048]{1,0:T(8,128)} convert(bf16[128,2048]{1,0:T(8,128)(2,1)} %param.7) | non-fusion elementwise | flops 262144 | bytes 1572864 | tf_op jit(solution)/shard_map/convert_element_type | solution.py:39
  103.9 47.6 %all-to-all-done = bf16[32,10,2048]{2,1,0:T(8,128)(2,1)} async-done(((bf16[32,10,2048]{2,1,0:T(8,128)(2,1)}), bf16[32,10,2048]{2,1,0:T(8,128)(2,1)}, u32[]{:S(2)}, u32[]{:S(2)}) %all-to-all-start) | async-done | bytes 1310752 | tf_op jit(solution)/shard_map/all_to_all | solution.py:66
  151.5 4.1 %multiply_reduce_fusion = (f32[128,2]{0,1:T(2,128)}, bf16[128,2048]{1,0:T(8,128)(2,1)}) fusion(f32[128,2048]{1,0:T(8,128)} %convert_element_type.56, f32[128,2]{0,1:T(2,128)S(1)} %copy-done.1, bf16[32,10,2048]{2,1,0:T(8,128)(2,1)} %all-to-all-done, s32[128,2]{0,1:T(2,128)S(1)} %multiply_add_fusion.2, s32[10,32]{1,0:T(8,128)S(1)} %multiply_add_fusion.1), kind=kOutput, calls=%fused_computation.9 | convolution fusion | flops 337460992 | bytes 2887936 | tf_op jit(solution)/shard_map/ecr,ecd->rd/dot_general | solution.py:67
  155.5 3.3 %fusion.13 = bf16[1,1,32,10,768]{4,2,3,1,0:T(8,128)(2,1)} fusion(bf16[32,10,2048]{2,0,1:T(8,128)(2,1)} %copy.43, bf16[1,768,2048]{2,1,0:T(8,128)(2,1)S(1)} %copy-done), kind=kOutput, calls=%fused_computation.14 | convolution fusion | flops 1006878720 | bytes 4947968 | tf_op jit(solution)/shard_map/scd,hd->sch/dot_general | solution.py:76
  158.9 16.9 %reduce-scatter.2.cloned.1.call-done = f32[24,2048]{1,0:T(8,128)} async-done(((f32[384,2048]{1,0:T(8,128)}), f32[24,2048]{1,0:T(8,128)}) %reduce-scatter.2.cloned.1.call-update) | async-done | bytes 196624 | tf_op jit(solution)/shard_map/reduce_scatter | solution.py:65
  (16 shorter events, 0.4 us)
Async XLA Ops:
  7.2 84.0 %copy-start = (bf16[1,768,2048]{2,1,0:T(8,128)(2,1)S(1)}, bf16[1,768,2048]{2,1,0:T(8,128)(2,1)}, u32[]{:S(2)}) copy-start(bf16[1,768,2048]{2,1,0:T(8,128)(2,1)} %param.8) | copy-start | bytes 9437188
  7.2 168.6 %reduce-scatter.2.cloned.1.call-start = ((), (), s32[]{:S(2)}) async-start(), calls=%async_computation.3 | async-start | bytes 3342336 | tf_op jit(solution)/shard_map/reduce_scatter | solution.py:65
  74.8 11.3 %collective-permute-start.1 = (bf16[32,10,2048]{2,0,1:T(8,128)(2,1)}, bf16[32,10,2048]{2,0,1:T(8,128)(2,1)}, u32[]{:S(2)}, u32[]{:S(2)}) collective-permute-start(bf16[32,10,2048]{2,0,1:T(8,128)(2,1)} %copy.43), channel_id=1, source_target_pairs={{0,32},{32,0},{1,33},{33,1},{2,34},{34,2},{3,35},{35,3},{4,36},{36... | collective-permute-start | bytes 3932168 | tf_op jit(solution)/shard_map/ppermute | solution.py:60
  79.0 7.1 %collective-permute-start = (bf16[32,10,384]{2,0,1:T(8,128)(2,1)}, bf16[32,10,384]{2,0,1:T(8,128)(2,1)S(1)}, u32[]{:S(2)}, u32[]{:S(2)}) collective-permute-start(bf16[32,10,384]{2,0,1:T(8,128)(2,1)} %fusion.23), channel_id=1, source_target_pairs={{0,32},{32,0},{1,33},{33,1},{2,34},{34,2},{3,35},{35,3},{4,36},{36... | collective-permute-start | bytes 737288 | tf_op jit(solution)/shard_map/ppermute | solution.py:59
  95.5 55.9 %copy-start.1 = (f32[128,2]{0,1:T(2,128)S(1)}, f32[128,2]{0,1:T(2,128)}, u32[]{:S(2)}) copy-start(f32[128,2]{0,1:T(2,128)} %param.6) | copy-start | bytes 3076
  95.5 55.9 %all-to-all-start = ((bf16[32,10,2048]{2,1,0:T(8,128)(2,1)}), bf16[32,10,2048]{2,1,0:T(8,128)(2,1)}, u32[]{:S(2)}, u32[]{:S(2)}) async-start(bf16[32,10,2048]{2,1,0:T(8,128)(2,1)} %copy.40), calls=%async_computation | async-start | bytes 4194304 | tf_op jit(solution)/shard_map/all_to_all | solution.py:66
Sparse Core Ops, SparseCore 0:
  91.3 84.4 reduce-scatter.1
